TPU v7x, 256 devices: a whole 4x4x8 slice. The times are simulated.
256 devices in a mesh: tok: 64 (over x_hi, z, y), ffn: 4 (over x_lo, core).
Axes of the slice: x: 4 (x_hi: 2, x_lo: 2; x = x_hi * 2 + x_lo), y: 4, z: 8, core: 2. Of those that a mesh axis runs over, the one named last changes fastest.
Arguments:
- hidden: bfloat16 [65536, 8192], P('tok', 'ffn'), may hold values from -6 to 6
- down_weight: bfloat16 [2, 3072, 8192], P(None, 'tok', 'ffn'), may hold values from -0.0625 to 0.0625
- block_expert: int32 [512], P('tok'), may hold values from 0 to 1, as said below
- slot_token: int32 [65536], P('tok'), may hold values from 0 to 512, as said below
- slot_weight: float32 [65536], P('tok'), may hold values from 0.1 to 1
Outputs:
- mixed: bfloat16 [32768, 3072], P('tok', 'ffn')
Inputs may be any that keep to these rules, and one draw needn't show every extreme that they name: `slot_token`: within each index of tok, slots 128 * b to 128 * b + 127 belong to expert block_expert of block b; each expert's blocks are consecutive, in expert order, with its live slots first; live slots of one expert hold distinct tokens; the value 512 marks an empty slot; one index of tok has at most 512 live slots for one expert, and for every expert some index has exactly that many. `block_expert`: every expert owns at least one block of every index of tok; blocks after the last expert's live slots carry the last expert.
All inputs are finite; a program needn't handle non-finite values.
Results may differ from a plain program's by a relative error of at most 0.001.
Values may be sent and summed in bfloat16 or wider, within the bound.
No kernel may reach another device: no remote copies, remote signals or barrier semaphores. Data moves between devices by JAX's collectives and lax.ppermute only.
A program may use at most 128 MiB of HBM per device.

v0:
```python
from functools import partial

import jax
import jax.numpy as jnp
from jax import lax
from jax.sharding import PartitionSpec as P

EXP = 2
BLOCK = 128
TOK_DEV = 512


def dot_with(number, hblock, w_piece):
    return lax.dot_general(
        hblock, w_piece[number], (((1,), (1,)), ((), ())), preferred_element_type=jnp.float32
    )


def local(hidden, down_weight, block_expert, slot_token, slot_weight):
    block_count = block_expert.shape[0]
    w_piece = lax.all_gather(down_weight, "tok", axis=1, tiled=True)
    block_outs = []
    for block_idx in range(block_count):
        hblock = hidden[block_idx * BLOCK : (block_idx + 1) * BLOCK]
        branches = [partial(dot_with, number) for number in range(EXP)]
        block_outs.append(lax.switch(block_expert[block_idx], branches, hblock, w_piece))
    slot_out = jnp.concatenate(block_outs, axis=0)
    is_live = slot_token < TOK_DEV
    slot_scale = jnp.where(is_live, slot_weight, jnp.zeros_like(slot_weight))
    token_slot = jnp.minimum(slot_token, TOK_DEV - 1)
    token_terms = jax.ops.segment_sum(
        slot_scale[:, None] * slot_out, token_slot, num_segments=TOK_DEV
    )
    mixed = lax.psum_scatter(token_terms, "ffn", scatter_dimension=1, tiled=True)
    return mixed.astype(jnp.bfloat16)


def solution(mesh):
    placed = (P("tok", "ffn"), P(None, "tok", "ffn"), P("tok"), P("tok"), P("tok"))
    return jax.shard_map(
        local, mesh=mesh, in_specs=placed, out_specs=P("tok", "ffn"), check_vma=False
    )
```

profile of v0, /device:TPU:1, one launch (start us, length us, event | category | flops | bytes accessed | tf_op | source)
XLA Modules:
  0.0 471.7 jit_solution(15124485633004217229)
XLA Ops:
  6.5 0.0 all-gather.2.cloned.1.call-start
  6.5 0.7 all-gather.2.cloned.1.call-update
  7.3 0.0 reduce-scatter.2.cloned.1.call-start
  7.3 1.6 fusion.53
  14.0 0.7 broadcast_minimum_fusion
  14.7 0.7 compare_select_fusion
  15.4 3.9 fusion.52
  19.3 268.5 %all-gather.2.cloned.1.call-done = bf16[2,3072,2048]{2,1,0:T(8,128)(2,1)} async-done(((bf16[2,48,2048]{2,1,0:T(8,128)(2,1)}), bf16[2,3072,2048]{2,1,0:T(8,128)(2,1)}) %all-gather.2.cloned.1.call-update) | async-done | bytes 25165840 | tf_op jit(solution)/shard_map/all_gather | solution.py:21
  287.8 7.2 %conditional.8 = (f32[128,3072]{1,0:T(8,128)S(1)}) conditional(s32[]{:T(128)} %bitcast.16, (bf16[2,3072,2048]{2,1,0:T(8,128)(2,1)}, bf16[128,2048]{1,0:T(8,128)(2,1)S(1)}) %tuple.53, (bf16[2,3072,2048]{2,1,0:T(8,128)(2,1)}, bf16[128,2048]{1,0:T(8,128)(2,1)S(1)}) %tuple.53), branch_computations={%region_0.0_spmd, %region_1.0_spmd} | conditional | flops 1610612736 | bytes 14680072 | solution.py:26
  287.8 7.2 %fusion = f32[128,3072]{1,0:T(8,128)S(1)} fusion(bf16[128,2048]{1,0:T(8,128)(2,1)S(1)} %get-tuple-element.85, bf16[2,3072,2048]{2,1,0:T(8,128)(2,1)} %get-tuple-element.86), kind=kOutput, calls=%fused_computation.1 | convolution fusion | flops 1610612736 | bytes 14680064 | tf_op jit(solution)/shard_map/cond/branch_0_fun/dot_general | solution.py:14
  295.1 1.3 constant_dynamic-update-slice_fusion.7
  296.4 7.2 %conditional.14 = (f32[128,3072]{1,0:T(8,128)S(1)}) conditional(s32[]{:T(128)} %bitcast.22, (bf16[2,3072,2048]{2,1,0:T(8,128)(2,1)}, bf16[128,2048]{1,0:T(8,128)(2,1)S(1)}) %tuple.59, (bf16[2,3072,2048]{2,1,0:T(8,128)(2,1)}, bf16[128,2048]{1,0:T(8,128)(2,1)S(1)}) %tuple.59), branch_computations={%region_12.0_spmd, %region_13.0_spmd} | conditional | flops 1610612736 | bytes 14680072 | solution.py:26
  296.4 7.2 %fusion.39 = f32[128,3072]{1,0:T(8,128)S(1)} fusion(bf16[128,2048]{1,0:T(8,128)(2,1)S(1)} %get-tuple-element.119, bf16[2,3072,2048]{2,1,0:T(8,128)(2,1)} %get-tuple-element.120), kind=kOutput, calls=%fused_computation.40 | convolution fusion | flops 1610612736 | bytes 14680064 | tf_op jit(solution)/shard_map/cond/branch_1_fun/dot_general | solution.py:14
  303.6 7.3 %conditional.9 = (f32[128,3072]{1,0:T(8,128)S(1)}) conditional(s32[]{:T(128)} %bitcast.17, (bf16[2,3072,2048]{2,1,0:T(8,128)(2,1)}, bf16[128,2048]{1,0:T(8,128)(2,1)}) %tuple.54, (bf16[2,3072,2048]{2,1,0:T(8,128)(2,1)}, bf16[128,2048]{1,0:T(8,128)(2,1)}) %tuple.54), branch_computations={%region_2.0_spmd, %region_3.0_spmd} | conditional | flops 1610612736 | bytes 14680072 | solution.py:26
  303.6 7.3 %fusion.6 = f32[128,3072]{1,0:T(8,128)S(1)} fusion(bf16[128,2048]{1,0:T(8,128)(2,1)} %get-tuple-element.92, bf16[2,3072,2048]{2,1,0:T(8,128)(2,1)} %get-tuple-element.96), kind=kOutput, calls=%fused_computation.7 | convolution fusion | flops 1610612736 | bytes 14680064 | tf_op jit(solution)/shard_map/cond/branch_0_fun/dot_general | solution.py:14
  311.0 10.3 %conditional.10 = (f32[128,3072]{1,0:T(8,128)}) conditional(s32[]{:T(128)} %bitcast.18, (bf16[2,3072,2048]{2,1,0:T(8,128)(2,1)}, bf16[128,2048]{1,0:T(8,128)(2,1)}) %tuple.55, (bf16[2,3072,2048]{2,1,0:T(8,128)(2,1)}, bf16[128,2048]{1,0:T(8,128)(2,1)}) %tuple.55), branch_computations={%region_4.0_spmd, %region_5.0_spmd} | conditional | flops 1610612736 | bytes 14680072 | solution.py:26
  311.2 10.2 %fusion.12 = f32[128,3072]{1,0:T(8,128)} fusion(bf16[128,2048]{1,0:T(8,128)(2,1)} %get-tuple-element.101, bf16[2,3072,2048]{2,1,0:T(8,128)(2,1)} %get-tuple-element.102), kind=kOutput, calls=%fused_computation.13 | convolution fusion | flops 1610612736 | bytes 14680064 | tf_op jit(solution)/shard_map/cond/branch_0_fun/dot_general | solution.py:14
  321.3 10.1 %conditional.11 = (f32[128,3072]{1,0:T(8,128)}) conditional(s32[]{:T(128)} %bitcast.19, (bf16[2,3072,2048]{2,1,0:T(8,128)(2,1)}, bf16[128,2048]{1,0:T(8,128)(2,1)}) %tuple.56, (bf16[2,3072,2048]{2,1,0:T(8,128)(2,1)}, bf16[128,2048]{1,0:T(8,128)(2,1)}) %tuple.56), branch_computations={%region_6.0_spmd, %region_7.0_spmd} | conditional | flops 1610612736 | bytes 14680072 | solution.py:26
  321.3 10.1 %fusion.21 = f32[128,3072]{1,0:T(8,128)} fusion(bf16[128,2048]{1,0:T(8,128)(2,1)} %get-tuple-element.107, bf16[2,3072,2048]{2,1,0:T(8,128)(2,1)} %get-tuple-element.108), kind=kOutput, calls=%fused_computation.22 | convolution fusion | flops 1610612736 | bytes 14680064 | tf_op jit(solution)/shard_map/cond/branch_1_fun/dot_general | solution.py:14
  331.5 10.6 %conditional.12 = (f32[128,3072]{1,0:T(8,128)}) conditional(s32[]{:T(128)} %bitcast.20, (bf16[2,3072,2048]{2,1,0:T(8,128)(2,1)}, bf16[128,2048]{1,0:T(8,128)(2,1)}) %tuple.57, (bf16[2,3072,2048]{2,1,0:T(8,128)(2,1)}, bf16[128,2048]{1,0:T(8,128)(2,1)}) %tuple.57), branch_computations={%region_8.0_spmd, %region_9.0_spmd} | conditional | flops 1610612736 | bytes 14680072 | solution.py:26
  331.8 10.2 %fusion.27 = f32[128,3072]{1,0:T(8,128)} fusion(bf16[128,2048]{1,0:T(8,128)(2,1)} %get-tuple-element.111, bf16[2,3072,2048]{2,1,0:T(8,128)(2,1)} %get-tuple-element.112), kind=kOutput, calls=%fused_computation.28 | convolution fusion | flops 1610612736 | bytes 14680064 | tf_op jit(solution)/shard_map/cond/branch_1_fun/dot_general | solution.py:14
  342.1 10.2 %conditional.13 = (f32[128,3072]{1,0:T(8,128)}) conditional(s32[]{:T(128)} %bitcast.21, (bf16[2,3072,2048]{2,1,0:T(8,128)(2,1)}, bf16[128,2048]{1,0:T(8,128)(2,1)}) %tuple.58, (bf16[2,3072,2048]{2,1,0:T(8,128)(2,1)}, bf16[128,2048]{1,0:T(8,128)(2,1)}) %tuple.58), branch_computations={%region_10.0_spmd, %region_11.0_spmd} | conditional | flops 1610612736 | bytes 14680072 | solution.py:26
  342.1 10.2 %fusion.33 = f32[128,3072]{1,0:T(8,128)} fusion(bf16[128,2048]{1,0:T(8,128)(2,1)} %get-tuple-element.115, bf16[2,3072,2048]{2,1,0:T(8,128)(2,1)} %get-tuple-element.116), kind=kOutput, calls=%fused_computation.34 | convolution fusion | flops 1610612736 | bytes 14680064 | tf_op jit(solution)/shard_map/cond/branch_1_fun/dot_general | solution.py:14
  352.3 10.3 %conditional.15 = (f32[128,3072]{1,0:T(8,128)}) conditional(s32[]{:T(128)} %bitcast.23, (bf16[2,3072,2048]{2,1,0:T(8,128)(2,1)}, bf16[128,2048]{1,0:T(8,128)(2,1)}) %tuple.60, (bf16[2,3072,2048]{2,1,0:T(8,128)(2,1)}, bf16[128,2048]{1,0:T(8,128)(2,1)}) %tuple.60), branch_computations={%region_14.0_spmd, %region_15.0_spmd} | conditional | flops 1610612736 | bytes 14680072 | solution.py:26
  352.5 10.2 %fusion.45 = f32[128,3072]{1,0:T(8,128)} fusion(bf16[128,2048]{1,0:T(8,128)(2,1)} %get-tuple-element.123, bf16[2,3072,2048]{2,1,0:T(8,128)(2,1)} %get-tuple-element.124), kind=kOutput, calls=%fused_computation.46 | convolution fusion | flops 1610612736 | bytes 14680064 | tf_op jit(solution)/shard_map/cond/branch_1_fun/dot_general | solution.py:14
  362.6 0.0 copy-start
  362.6 0.0 copy-start.1
  362.6 1.3 constant_dynamic-update-slice_fusion.6
  363.9 3.1 constant_dynamic-update-slice_fusion.5
  366.9 2.7 constant_dynamic-update-slice_fusion.4
  369.7 2.7 constant_dynamic-update-slice_fusion.3
  372.4 0.0 copy-done
  372.4 1.3 constant_dynamic-update-slice_fusion.2
  373.6 1.2 constant_dynamic-update-slice_fusion.1
  374.9 0.0 copy-done.1
  374.9 1.3 constant_dynamic-update-slice_fusion
  376.2 23.1 %scatter_custom_fusion = f32[512,3072]{1,0:T(8,128)} fusion(s32[1024]{0:T(1024)S(1)} %broadcast_minimum_fusion, f32[1024,3072]{1,0:T(8,128)} %constant_dynamic-update-slice_fusion, f32[1024]{0:T(1024)S(1)} %compare_select_fusion, f32[]{:T(128)} %constant.22.clone.1), kind=kCustom, calls=%fused_computation.49 | custom fusion | flops 6291456 | bytes 18878468 | tf_op jit(solution)/shard_map/scatter-add | solution.py:31
  399.3 0.0 reduce-scatter.2.cloned.1.call-update
  399.3 63.0 %reduce-scatter.2.cloned.1.call-done = f32[512,768]{1,0:T(8,128)} async-done(((f32[512,3072]{1,0:T(8,128)}), f32[512,768]{1,0:T(8,128)}) %reduce-scatter.2.cloned.1.call-update) | async-done | bytes 1572880 | tf_op jit(solution)/shard_map/reduce_scatter | solution.py:34
  462.3 2.4 convert_element_type.3
Async XLA Ops:
  6.5 281.3 %all-gather.2.cloned.1.call-start = ((), (), s32[]{:S(2)}) async-start(), calls=%async_computation.1 | async-start | bytes 25559040 | tf_op jit(solution)/shard_map/all_gather | solution.py:21
  7.3 455.0 %reduce-scatter.2.cloned.1.call-start = ((), (), s32[]{:S(2)}) async-start(), calls=%async_computation.2 | async-start | bytes 7864320 | tf_op jit(solution)/shard_map/reduce_scatter | solution.py:34
  362.6 9.7 %copy-start = (f32[128,3072]{1,0:T(8,128)S(1)}, f32[128,3072]{1,0:T(8,128)}, u32[]{:S(2)}) copy-start(f32[128,3072]{1,0:T(8,128)} %get-tuple-element.146) | copy-start | bytes 4718596
  362.6 12.2 %copy-start.1 = (f32[128,3072]{1,0:T(8,128)S(1)}, f32[128,3072]{1,0:T(8,128)}, u32[]{:S(2)}) copy-start(f32[128,3072]{1,0:T(8,128)} %get-tuple-element.148) | copy-start | bytes 4718596
Sparse Core Ops, SparseCore 0:
  11.0 276.7 all-gather.1
  399.5 62.8 reduce-scatter.1
where the time goes:
time: 479 us; the launch traced here: 472 us
  waiting for transfers between devices  332 us (69%)
  matrix products  72.7 us (15%)
  other arithmetic  26.9 us (6%)
  local copies, waits for them, and re-layouts  20.4 us (4%)
  between operations  18.7 us (4%)
    all_gather x1, waiting for transfers between devices, local(): w_piece = lax.all_gather(down_weight, 'tok', axis=1, tiled=True)  268 us
    dot_general x8, matrix products, dot_with(): lax.dot_general(hblock, w_piece[number], (((1,), (1,)), ((), ())), prefer...  72.7 us
    reduce_scatter x1, waiting for transfers between devices, local(): lax.psum_scatter(token_terms, 'ffn', scatter_dimension=1, tiled=True)  63 us
    scatter-add x1, other arithmetic, local(): jax.ops.segment_sum(slot_scale[:, None] * slot_out, token_slot, num_segme...  23.1 us
    unnamed x11, local copies, waits for them, and re-layouts  13.6 us
  transfers between devices with their start and end apart: 2, of which 2 were waited for; matrix products, arithmetic and copies ran while one was open for 1% of the time, Pallas kernels for 0%

commit v1 on v0

v1 whole, which is shorter than its diff:
```python
import jax
import jax.numpy as jnp
from jax import lax
from jax.sharding import Mesh, PartitionSpec as P

EXP = 2
BLOCK = 128
TOK_DEV = 512

TOK = ("xh", "z", "y")
FFN = ("xl", "c")


def local(hidden, down_weight, block_expert, slot_token, slot_weight):
    halves = lax.all_gather(down_weight, "xh", axis=0, tiled=False)
    w_full = lax.all_gather(halves, ("z", "y"), axis=2, tiled=True)
    slot_expert = jnp.repeat(block_expert, BLOCK)
    tokens = jnp.arange(TOK_DEV, dtype=jnp.int32)
    same_token = slot_token[None, :] == tokens[:, None]
    token_terms = None
    for number in range(EXP):
        pick = same_token & (slot_expert == number)[None, :]
        scale = jnp.sum(jnp.where(pick, slot_weight[None, :], 0.0), axis=1)
        rows = lax.dot_general(
            pick.astype(hidden.dtype), hidden, (((1,), (0,)), ((), ())),
            preferred_element_type=jnp.float32,
        ).astype(hidden.dtype)
        out = lax.dot_general(
            rows, w_full[:, number], (((1,), (2,)), ((), ())),
            preferred_element_type=jnp.float32,
        )
        term = scale[:, None] * out.reshape(TOK_DEV, -1)
        token_terms = term if token_terms is None else token_terms + term
    mixed = lax.psum_scatter(token_terms, FFN, scatter_dimension=1, tiled=True)
    return mixed.astype(jnp.bfloat16)


def solution(mesh):
    tok_size, ffn_size = mesh.devices.shape
    fine = Mesh(mesh.devices.reshape(2, tok_size // 8, 4, 2, ffn_size // 2), TOK + FFN)
    placed = (P(TOK, FFN), P(None, TOK, FFN), P(TOK), P(TOK), P(TOK))
    return jax.shard_map(
        local, mesh=fine, in_specs=placed, out_specs=P(TOK, FFN), check_vma=False
    )
```

time: 479 us -> 322 us (0.67); the launches traced: 472 us -> 321 us
  waiting for transfers between devices: 332 us -> 241 us
  matrix products: 72.7 us -> 31.1 us
  other arithmetic: 26.9 us -> 4.59 us
  blocking collectives: 0 us -> 17.2 us
  local copies, waits for them, and re-layouts: 20.4 us -> 13.9 us
  between operations: 18.7 us -> 13.4 us
    all_gather x1, waiting for transfers between devices: 268 us -> 178 us  [local(): w_full = lax.all_gather(halves, ('z', 'y'), axis=2, tiled=True)]
    dot_general x8 -> x3, matrix products: 72.7 us -> 31.1 us  [the longest x2 26.6 us: local(): lax.dot_general(rows, w_full[:, number], (((1,), (2,)), ((), ())), prefer...]
    scatter-add x1 -> x0, other arithmetic: 23.1 us -> none  [local(): jax.ops.segment_sum(slot_scale[:, None] * slot_out, token_slot, num_segme...]
    all_gather x0 -> x1, blocking collectives: none -> 17.2 us  [local(): halves = lax.all_gather(down_weight, 'xh', axis=0, tiled=False)]
    unnamed x11 -> x2, local copies, waits for them, and re-layouts: 13.6 us -> 0.01 us
    slice x2 -> x1, local copies, waits for them, and re-layouts: 5.54 us -> 13.8 us  [local(): w_full[:, number]]
  transfers between devices with their start and end apart: 2 -> 2, of which waited for: 2 -> 2; matrix products, arithmetic and copies ran while one was open for 1% -> 2% of each run, Pallas kernels for 0% -> 0%
where the time goes in v1:
time: 322 us; the launch traced here: 321 us
  waiting for transfers between devices  241 us (75%)
  matrix products  31.1 us (10%)
  blocking collectives  17.2 us (5%)
  local copies, waits for them, and re-layouts  13.9 us (4%)
  between operations  13.4 us (4%)
  other arithmetic  4.59 us (1%)
    all_gather x1, waiting for transfers between devices, local(): w_full = lax.all_gather(halves, ('z', 'y'), axis=2, tiled=True)  178 us
    reduce_scatter x1, waiting for transfers between devices, local(): mixed = lax.psum_scatter(token_terms, FFN, scatter_dimension=1, tiled=True)  63.2 us
    dot_general x2, matrix products, local(): lax.dot_general(rows, w_full[:, number], (((1,), (2,)), ((), ())), prefer...  26.6 us
    all_gather x1, blocking collectives, local(): halves = lax.all_gather(down_weight, 'xh', axis=0, tiled=False)  17.2 us
    slice x1, local copies, waits for them, and re-layouts, local(): w_full[:, number]  13.8 us
  transfers between devices with their start and end apart: 2, of which 2 were waited for; matrix products, arithmetic and copies ran while one was open for 2% of the time, Pallas kernels for 0%

profile of v1, /device:TPU:1, one launch (start us, length us, event | category | flops | bytes accessed | tf_op | source)
XLA Modules:
  0.0 321.1 jit_solution(18043190102445400774)
XLA Ops:
  6.5 0.0 all-gather.3.cloned.1.call-start
  6.5 17.2 %all-gather = bf16[4,48,2048]{2,1,0:T(8,128)(2,1)} all-gather(bf16[2,48,2048]{2,1,0:T(8,128)(2,1)} %param.6), channel_id=2, replica_groups=mesh['xh'=2,'z'=8,'y'=4,'xl'=2,'c'=2] {'xh'}, dimensions={0}, use_global_device_ids=true | all-gather | bytes 1179648 | tf_op jit(solution)/shard_map/all_gather | solution.py:15
  23.7 0.0 all-gather.3.cloned.1.call-update
  23.7 0.0 reduce-scatter.2.cloned.1.call-start
  23.8 0.7 broadcast_compare_fusion
  24.4 0.1 broadcast_bitcast_fusion
  24.5 1.6 select_reduce_fusion.1
  26.1 4.5 %convolution_convert_fusion.1 = bf16[512,2048]{1,0:T(8,128)(2,1)S(1)} fusion(bf16[1024,2048]{1,0:T(8,128)(2,1)} %param.5, s32[1024]{0:T(1024)} %param.8, pred[1024]{0:T(1024)(128)(4,1)S(1)} %get-tuple-element.12), kind=kOutput, calls=%fused_computation.2 | convolution fusion | flops 2149580800 | bytes 6296576 | tf_op jit(solution)/shard_map/dot_general | solution.py:24
  30.6 177.7 %all-gather.3.cloned.1.call-done = bf16[2,2,1536,2048]{3,2,1,0:T(8,128)(2,1)} async-done(((bf16[2,2,48,2048]{3,2,1,0:T(8,128)(2,1)}), bf16[2,2,1536,2048]{3,2,1,0:T(8,128)(2,1)}) %all-gather.3.cloned.1.call-update) | async-done | bytes 25165840 | tf_op jit(solution)/shard_map/all_gather | solution.py:16
  208.3 13.8 %fusion.8 = (bf16[2,1,1536,2048]{3,2,1,0:T(8,128)(2,1)}, bf16[2,1,1536,2048]{3,2,1,0:T(8,128)(2,1)S(1)}) fusion(bf16[2,2,1536,2048]{3,2,1,0:T(8,128)(2,1)} %all-gather.3.cloned.1.call-done), kind=kLoop, calls=%fused_computation.16 | loop fusion | bytes 50331648 | tf_op jit(solution)/shard_map/slice | solution.py:29
  222.1 0.0 copy-start
  222.1 8.8 %fusion.9 = f32[512,3072]{1,0:T(8,128)} fusion(bf16[512,2048]{1,0:T(8,128)(2,1)S(1)} %convolution_convert_fusion.1, bf16[3072,2048]{1,0:T(8,128)(2,1)S(1)} %bitcast.18), kind=kOutput, calls=%fused_computation.17 | convolution fusion | flops 6442450944 | bytes 20971520 | tf_op jit(solution)/shard_map/dot_general | solution.py:28
  230.9 0.0 copy-done
  230.9 17.8 %multiply_add_fusion = f32[512,3072]{1,0:T(8,128)} fusion(f32[512,3072]{1,0:T(8,128)} %fusion.9, bf16[3072,2048]{1,0:T(8,128)(2,1)} %bitcast.17, f32[512]{0:T(512)S(1)} %get-tuple-element.6, f32[512]{0:T(512)S(1)} %get-tuple-element.5, bf16[1024,2048]{1,0:T(8,128)(2,1)} %param.5, s32[1024]{0:T(1024)S(1)} %copy-done, pred[1024]{0:T(1024)(128)(4,1)S(1)} %get-tuple-element.11), kind=kOutput, calls=%fused_computation | convolution fusion | flops 8596750336 | bytes 29369344 | tf_op jit(solution)/shard_map/dot_general | solution.py:28
  248.7 0.0 reduce-scatter.2.cloned.1.call-update
  248.8 63.2 %reduce-scatter.2.cloned.1.call-done = f32[512,768]{1,0:T(8,128)} async-done(((f32[512,3072]{1,0:T(8,128)}), f32[512,768]{1,0:T(8,128)}) %reduce-scatter.2.cloned.1.call-update) | async-done | bytes 1572880 | tf_op jit(solution)/shard_map/reduce_scatter | solution.py:34
  311.9 2.4 convert_element_type.13
Async XLA Ops:
  6.5 201.8 %all-gather.3.cloned.1.call-start = ((), (), s32[]{:S(2)}) async-start(), calls=%async_computation.1 | async-start | bytes 25952256 | tf_op jit(solution)/shard_map/all_gather | solution.py:16
  23.7 288.2 %reduce-scatter.2.cloned.1.call-start = ((), (), s32[]{:S(2)}) async-start(), calls=%async_computation.2 | async-start | bytes 7864320 | tf_op jit(solution)/shard_map/reduce_scatter | solution.py:34
  222.1 8.8 %copy-start = (s32[1024]{0:T(1024)S(1)}, s32[1024]{0:T(1024)}, u32[]{:S(2)}) copy-start(s32[1024]{0:T(1024)} %param.8) | copy-start | bytes 12292
Sparse Core Ops, SparseCore 0:
  23.8 184.4 all-gather.2
  248.9 63.0 reduce-scatter.1

commit v2 on v1

v2 whole, which is shorter than its diff:
```python
import jax
import jax.numpy as jnp
from jax import lax
from jax.sharding import Mesh, PartitionSpec as P

EXP = 2
BLOCK = 128
TOK_DEV = 512

TOK = ("xh", "z", "y")
FFN = ("xl", "c")


def half_terms(rows, scale, w_half):
    out = lax.dot_general(
        rows, w_half, (((2,), (2,)), ((0,), (0,))), preferred_element_type=jnp.float32
    )
    return jnp.sum(scale[:, :, None] * out, axis=0)


def local(hidden, down_weight, block_expert, slot_token, slot_weight):
    own_half = lax.all_gather(down_weight, ("z", "y"), axis=1, tiled=True)
    partner = lax.ppermute(down_weight, "xh", perm=[(0, 1), (1, 0)])
    other_half = lax.all_gather(partner, ("z", "y"), axis=1, tiled=True)
    slot_expert = jnp.repeat(block_expert, BLOCK)
    tokens = jnp.arange(TOK_DEV, dtype=jnp.int32)
    experts = jnp.arange(EXP, dtype=jnp.int32)
    pick = (slot_token[None, None, :] == tokens[None, :, None]) & (
        slot_expert[None, None, :] == experts[:, None, None]
    )
    scale = jnp.sum(jnp.where(pick, slot_weight[None, None, :], 0.0), axis=2)
    rows = lax.dot_general(
        pick.astype(hidden.dtype), hidden, (((2,), (0,)), ((), ())),
        preferred_element_type=jnp.float32,
    ).astype(hidden.dtype)
    own_terms = half_terms(rows, scale, own_half)
    other_terms = half_terms(rows, scale, other_half)
    first = lax.axis_index("xh") == 0
    token_terms = jnp.concatenate(
        [jnp.where(first, own_terms, other_terms), jnp.where(first, other_terms, own_terms)], axis=1
    )
    mixed = lax.psum_scatter(token_terms, FFN, scatter_dimension=1, tiled=True)
    return mixed.astype(jnp.bfloat16)


def solution(mesh):
    tok_size, ffn_size = mesh.devices.shape
    fine = Mesh(mesh.devices.reshape(2, tok_size // 8, 4, 2, ffn_size // 2), TOK + FFN)
    placed = (P(TOK, FFN), P(None, TOK, FFN), P(TOK), P(TOK), P(TOK))
    return jax.shard_map(
        local, mesh=fine, in_specs=placed, out_specs=P(TOK, FFN), check_vma=False
    )
```

time: 322 us -> 338 us (1.050)
  waiting for transfers between devices: 241 us -> 280 us
  blocking collectives: 17.2 us -> 0 us
  local copies, waits for them, and re-layouts: 13.9 us -> 0.82 us
  other arithmetic: 4.59 us -> 8.79 us
  starting transfers between devices: 0.04 us -> 3.73 us
    all_gather x1 -> x2, waiting for transfers between devices: 178 us -> 208 us  [the longest x1 107 us: local(): other_half = lax.all_gather(partner, ('z', 'y'), axis=1, tiled=True)]
    all_gather x1 -> x0, blocking collectives: 17.2 us -> none  [local(): halves = lax.all_gather(down_weight, 'xh', axis=0, tiled=False)]
    slice x1 -> x0, local copies, waits for them, and re-layouts: 13.8 us -> none  [local(): w_full[:, number]]
    ppermute x0 -> x1, waiting for transfers between devices: none -> 8.11 us  [local(): partner = lax.ppermute(down_weight, 'xh', perm=[(0, 1), (1, 0)])]
    ppermute x0 -> x1, starting transfers between devices: none -> 3.65 us  [local(): partner = lax.ppermute(down_weight, 'xh', perm=[(0, 1), (1, 0)])]
  transfers between devices with their start and end apart: 2 -> 4, of which waited for: 2 -> 4; matrix products, arithmetic and copies ran while one was open for 2% -> 7% of each run, Pallas kernels for 0% -> 0%
where the time goes in v2:
time: 338 us
  waiting for transfers between devices  280 us (83%)
  matrix products  30.8 us (9%)
  between operations  13.2 us (4%)
  other arithmetic  8.79 us (3%)
  starting transfers between devices  3.73 us (1%)
    all_gather x1, waiting for transfers between devices, local(): other_half = lax.all_gather(partner, ('z', 'y'), axis=1, tiled=True)  107 us
    all_gather x1, waiting for transfers between devices, local(): own_half = lax.all_gather(down_weight, ('z', 'y'), axis=1, tiled=True)  101 us
    reduce_scatter x1, waiting for transfers between devices, local(): mixed = lax.psum_scatter(token_terms, FFN, scatter_dimension=1, tiled=True)  63.2 us
    dot_general x2, matrix products, half_terms(): lax.dot_general(rows, w_half, (((2,), (2,)), ((0,), (0,))), preferred_ele...  22.6 us
    dot_general x1, matrix products, local(): lax.dot_general(pick.astype(hidden.dtype), hidden, (((2,), (0,)), ((), ()...  8.2 us
    ppermute x1, waiting for transfers between devices, local(): partner = lax.ppermute(down_weight, 'xh', perm=[(0, 1), (1, 0)])  8.11 us
  transfers between devices with their start and end apart: 4, of which 4 were waited for; matrix products, arithmetic and copies ran while one was open for 7% of the time, Pallas kernels for 0%

profile of v2, /device:TPU:1, one launch (start us, length us, event | category | flops | bytes accessed | tf_op | source)
XLA Modules:
  0.0 337.6 jit_solution(9834018968012092343)
XLA Ops:
  6.5 0.0 copy-start
  6.5 0.0 all-gather.3.cloned.1.call-start
  6.5 0.7 all-gather.3.cloned.1.call-update
  7.3 0.0 all-gather.5.cloned.1.call-start
  7.3 3.6 %collective-permute-start = (bf16[2,48,2048]{2,1,0:T(8,128)(2,1)}, bf16[2,48,2048]{2,1,0:T(8,128)(2,1)S(1)}, u32[]{:S(2)}, u32[]{:S(2)}) collective-permute-start(bf16[2,48,2048]{2,1,0:T(8,128)(2,1)} %param.6), channel_id=1, source_target_pairs={{0,128},{128,0},{1,129},{129,1},{2,130},{130,2},{3,131},{131,3},{4... | collective-permute-start | bytes 1179656 | tf_op jit(solution)/shard_map/ppermute | solution.py:23
  11.0 8.1 %collective-permute-done = bf16[2,48,2048]{2,1,0:T(8,128)(2,1)S(1)} collective-permute-done((bf16[2,48,2048]{2,1,0:T(8,128)(2,1)}, bf16[2,48,2048]{2,1,0:T(8,128)(2,1)S(1)}, u32[]{:S(2)}, u32[]{:S(2)}) %collective-permute-start) | collective-permute-done | bytes 393248 | tf_op jit(solution)/shard_map/ppermute | solution.py:23
  19.1 0.0 copy-start.1
  19.1 0.7 copy-done.1
  19.8 0.0 all-gather.5.cloned.1.call-update
  19.8 0.0 reduce-scatter.2.cloned.1.call-start
  19.9 0.0 copy-done
  19.9 0.1 broadcast_bitcast_fusion
  20.0 1.0 iota_compare_fusion
  21.0 1.5 fusion.2
  22.5 8.2 %fusion.4 = bf16[2,512,2048]{2,1,0:T(8,128)(2,1)} fusion(bf16[1024,2048]{1,0:T(8,128)(2,1)} %param.5, pred[2,1024]{1,0:T(4,128)(4,1)S(1)} %iota_compare_fusion.1, pred[512,1024]{1,0:T(8,128)(4,1)S(1)} %iota_compare_fusion), kind=kOutput, calls=%fused_computation.8 | convolution fusion | flops 4298113024 | bytes 8914944 | tf_op jit(solution)/shard_map/dot_general | solution.py:32
  30.7 101.1 %all-gather.3.cloned.1.call-done = bf16[2,1536,2048]{2,1,0:T(8,128)(2,1)} async-done(((bf16[2,48,2048]{2,1,0:T(8,128)(2,1)}), bf16[2,1536,2048]{2,1,0:T(8,128)(2,1)}) %all-gather.3.cloned.1.call-update) | async-done | bytes 12582928 | tf_op jit(solution)/shard_map/all_gather | solution.py:22
  131.8 11.3 %multiply_reduce_fusion.1 = f32[512,1536]{1,0:T(8,128)S(1)} fusion(bf16[2,512,2048]{2,1,0:T(8,128)(2,1)} %fusion.4, bf16[2,1536,2048]{2,1,0:T(8,128)(2,1)} %all-gather.3.cloned.1.call-done, f32[2,512]{1,0:T(2,128)S(1)} %fusion.2), kind=kOutput, calls=%fused_computation.2 | convolution fusion | flops 6444810240 | bytes 19927040 | tf_op jit(solution)/shard_map/dot_general | solution.py:15
  143.1 107.2 %all-gather.5.cloned.1.call-done = bf16[2,1536,2048]{2,1,0:T(8,128)(2,1)} async-done(((bf16[2,48,2048]{2,1,0:T(8,128)(2,1)}), bf16[2,1536,2048]{2,1,0:T(8,128)(2,1)}) %all-gather.5.cloned.1.call-update) | async-done | bytes 12582928 | tf_op jit(solution)/shard_map/all_gather | solution.py:24
  250.3 11.3 %multiply_reduce_fusion = f32[512,1536]{1,0:T(8,128)S(1)} fusion(bf16[2,512,2048]{2,1,0:T(8,128)(2,1)} %fusion.4, bf16[2,1536,2048]{2,1,0:T(8,128)(2,1)} %all-gather.5.cloned.1.call-done, f32[2,512]{1,0:T(2,128)S(1)} %fusion.2), kind=kOutput, calls=%fused_computation.1 | convolution fusion | flops 6444810240 | bytes 19927040 | tf_op jit(solution)/shard_map/dot_general | solution.py:15
  261.6 0.7 broadcast_select_fusion.1
  262.3 3.2 pad_maximum_fusion
  265.5 0.0 reduce-scatter.2.cloned.1.call-update
  265.5 63.2 %reduce-scatter.2.cloned.1.call-done = f32[512,768]{1,0:T(8,128)} async-done(((f32[512,3072]{1,0:T(8,128)}), f32[512,768]{1,0:T(8,128)}) %reduce-scatter.2.cloned.1.call-update) | async-done | bytes 1572880 | tf_op jit(solution)/shard_map/reduce_scatter | solution.py:42
  328.7 2.4 convert_element_type.8
  (1 shorter events, 0.0 us)
Async XLA Ops:
  6.5 13.4 %copy-start = (s32[8]{0:T(128)S(1)}, s32[8]{0:T(128)}, u32[]{:S(2)}) copy-start(s32[8]{0:T(128)} %param.7) | copy-start | bytes 100
  6.5 125.3 %all-gather.3.cloned.1.call-start = ((), (), s32[]{:S(2)}) async-start(), calls=%async_computation.1 | async-start | bytes 12976128 | tf_op jit(solution)/shard_map/all_gather | solution.py:22
  7.3 243.0 %all-gather.5.cloned.1.call-start = ((), (), s32[]{:S(2)}) async-start(), calls=%async_computation.2 | async-start | bytes 12976128 | tf_op jit(solution)/shard_map/all_gather | solution.py:24
  7.3 11.8 %collective-permute-start = (bf16[2,48,2048]{2,1,0:T(8,128)(2,1)}, bf16[2,48,2048]{2,1,0:T(8,128)(2,1)S(1)}, u32[]{:S(2)}, u32[]{:S(2)}) collective-permute-start(bf16[2,48,2048]{2,1,0:T(8,128)(2,1)} %param.6), channel_id=1, source_target_pairs={{0,128},{128,0},{1,129},{129,1},{2,130},{130,2},{3,131},{131,3},{4... | collective-permute-start | bytes 1179656 | tf_op jit(solution)/shard_map/ppermute | solution.py:23
  19.1 0.7 copy-start.1
  19.8 308.9 %reduce-scatter.2.cloned.1.call-start = ((), (), s32[]{:S(2)}) async-start(), calls=%async_computation.3 | async-start | bytes 7864320 | tf_op jit(solution)/shard_map/reduce_scatter | solution.py:42
Sparse Core Ops, SparseCore 0:
  9.9 121.8 all-gather.2
  134.4 115.8 all-gather.4
  265.6 63.0 reduce-scatter.1

commit v3 on v2

v3 whole, which is shorter than its diff:
```python
import jax
import jax.numpy as jnp
from jax import lax
from jax.sharding import Mesh, PartitionSpec as P

EXP = 2
BLOCK = 128
TOK_DEV = 512

TOK = ("xh", "z", "y")
FFN = ("xl", "c")
SWAP = [(0, 1), (1, 0)]


def halve(terms, axis, name):
    own = lax.axis_index(name)
    keep = lax.dynamic_index_in_dim(terms, own, axis=axis, keepdims=False)
    send = lax.dynamic_index_in_dim(terms, 1 - own, axis=axis, keepdims=False)
    return keep + lax.ppermute(send, name, perm=SWAP)


def local(hidden, down_weight, block_expert, slot_token, slot_weight):
    partner = lax.ppermute(down_weight, "xh", perm=SWAP)
    first = lax.axis_index("xh") == 0
    pair = jnp.stack(
        [jnp.where(first, down_weight, partner), jnp.where(first, partner, down_weight)], axis=0
    )
    w_full = lax.all_gather(pair, ("z", "y"), axis=2, tiled=True)
    slot_expert = jnp.repeat(block_expert, BLOCK)
    tokens = jnp.arange(TOK_DEV, dtype=jnp.int32)
    experts = jnp.arange(EXP, dtype=jnp.int32)
    pick = (slot_token[None, None, :] == tokens[None, :, None]) & (
        slot_expert[None, None, :] == experts[:, None, None]
    )
    scale = jnp.sum(jnp.where(pick, slot_weight[None, None, :], 0.0), axis=2)
    rows = lax.dot_general(
        pick.astype(hidden.dtype), hidden, (((2,), (0,)), ((), ())),
        preferred_element_type=jnp.float32,
    ).astype(hidden.dtype)
    out = lax.dot_general(
        rows, w_full, (((2,), (3,)), ((0,), (1,))), preferred_element_type=jnp.float32
    )
    token_terms = jnp.sum(scale[:, :, None, None] * out, axis=0)
    half = token_terms.shape[2]
    token_terms = token_terms.reshape(TOK_DEV, 2, 2, half // 2).transpose(1, 2, 0, 3)
    mixed = halve(halve(token_terms, 1, "c"), 0, "xl")
    return mixed.astype(jnp.bfloat16)


def solution(mesh):
    tok_size, ffn_size = mesh.devices.shape
    fine = Mesh(mesh.devices.reshape(2, tok_size // 8, 4, 2, ffn_size // 2), TOK + FFN)
    placed = (P(TOK, FFN), P(None, TOK, FFN), P(TOK), P(TOK), P(TOK))
    return jax.shard_map(
        local, mesh=fine, in_specs=placed, out_specs=P(TOK, FFN), check_vma=False
    )
```

time: 338 us -> 304 us (0.90)
  waiting for transfers between devices: 280 us -> 233 us
  local copies, waits for them, and re-layouts: 0.82 us -> 11.3 us
    reduce_scatter x1 -> x0, waiting for transfers between devices: 63.2 us -> none  [local(): mixed = lax.psum_scatter(token_terms, FFN, scatter_dimension=1, tiled=True)]
    ppermute x1 -> x3, waiting for transfers between devices: 8.11 us -> 47.8 us  [the longest x2 39.7 us: halve(): return keep + lax.ppermute(send, name, perm=SWAP)]
    all_gather x2 -> x1, waiting for transfers between devices: 208 us -> 186 us  [local(): w_full = lax.all_gather(pair, ('z', 'y'), axis=2, tiled=True)]
    reduce_sum x0 -> x1, local copies, waits for them, and re-layouts: none -> 6.57 us  [local(): token_terms = jnp.sum(scale[:, :, None, None] * out, axis=0)]
    add x0 -> x1, other arithmetic: none -> 3.59 us  [halve(): return keep + lax.ppermute(send, name, perm=SWAP)]
    dot_general x3 -> x1, matrix products: 30.8 us -> 29.8 us  [local(): lax.dot_general(rows, w_full, (((2,), (3,)), ((0,), (1,))), preferred_ele...]
  transfers between devices with their start and end apart: 4 -> 4, of which waited for: 4 -> 4; matrix products, arithmetic and copies ran while one was open for 7% -> 1% of each run, Pallas kernels for 0% -> 0%
where the time goes in v3:
time: 304 us
  waiting for transfers between devices  233 us (77%)
  matrix products  29.8 us (10%)
  between operations  13.4 us (4%)
  local copies, waits for them, and re-layouts  11.3 us (4%)
  other arithmetic  10 us (3%)
  starting transfers between devices  6.24 us (2%)
    all_gather x1, waiting for transfers between devices, local(): w_full = lax.all_gather(pair, ('z', 'y'), axis=2, tiled=True)  186 us
    ppermute x2, waiting for transfers between devices, halve(): return keep + lax.ppermute(send, name, perm=SWAP)  39.7 us
    dot_general x1, matrix products, local(): lax.dot_general(rows, w_full, (((2,), (3,)), ((0,), (1,))), preferred_ele...  29.8 us
    ppermute x1, waiting for transfers between devices, local(): partner = lax.ppermute(down_weight, 'xh', perm=SWAP)  8.11 us
    reduce_sum x1, local copies, waits for them, and re-layouts, local(): token_terms = jnp.sum(scale[:, :, None, None] * out, axis=0)  6.57 us
  transfers between devices with their start and end apart: 4, of which 4 were waited for; matrix products, arithmetic and copies ran while one was open for 1% of the time, Pallas kernels for 0%

profile of v3, /device:TPU:1, one launch (start us, length us, event | category | flops | bytes accessed | tf_op | source)
XLA Modules:
  0.0 304.2 jit_solution(11272980308769807626)
XLA Ops:
  6.5 0.0 copy-start
  6.5 0.0 copy-start.1
  6.5 0.0 all-gather.2.cloned.1.call-start
  6.5 3.6 %collective-permute-start = (bf16[2,48,2048]{2,1,0:T(8,128)(2,1)}, bf16[2,48,2048]{2,1,0:T(8,128)(2,1)S(1)}, u32[]{:S(2)}, u32[]{:S(2)}) collective-permute-start(bf16[2,48,2048]{2,1,0:T(8,128)(2,1)} %param.6), channel_id=1, source_target_pairs={{0,128},{128,0},{1,129},{129,1},{2,130},{130,2},{3,131},{131,3},{4... | collective-permute-start | bytes 1179656 | tf_op jit(solution)/shard_map/ppermute | solution.py:23
  10.1 8.1 %collective-permute-done = bf16[2,48,2048]{2,1,0:T(8,128)(2,1)S(1)} collective-permute-done((bf16[2,48,2048]{2,1,0:T(8,128)(2,1)}, bf16[2,48,2048]{2,1,0:T(8,128)(2,1)S(1)}, u32[]{:S(2)}, u32[]{:S(2)}) %collective-permute-start) | collective-permute-done | bytes 393248 | tf_op jit(solution)/shard_map/ppermute | solution.py:23
  18.2 1.1 select_bitcast_fusion.1
  19.3 0.9 pad_maximum_fusion
  20.3 0.0 all-gather.2.cloned.1.call-update
  20.3 0.0 copy-done
  20.3 0.1 broadcast_bitcast_fusion
  20.4 1.0 iota_compare_fusion
  21.4 0.0 copy-done.1
  21.4 0.8 fusion.2
  22.2 185.7 %all-gather.2.cloned.1.call-done = bf16[2,2,1536,2048]{3,2,0,1:T(8,128)(2,1)} async-done(((bf16[2,2,48,2048]{3,2,0,1:T(8,128)(2,1)}), bf16[2,2,1536,2048]{3,2,0,1:T(8,128)(2,1)}) %all-gather.2.cloned.1.call-update) | async-done | bytes 25165840 | tf_op jit(solution)/shard_map/all_gather | solution.py:28
  207.9 29.8 %multiply_reduce_fusion = f32[512,2,1536]{2,0,1:T(8,128)} fusion(bf16[2,2,1536,2048]{3,2,0,1:T(8,128)(2,1)} %all-gather.2.cloned.1.call-done, f32[2,512]{1,0:T(2,128)S(1)} %fusion.2, bf16[1024,2048]{1,0:T(8,128)(2,1)} %param.5, pred[2,1024]{1,0:T(4,128)(4,1)S(1)} %iota_compare_fusion.1, pred[512,1024]{1,0:T(8,128)(4,1)S(1)} %iota_compare_fusion), kind=kOutput, calls=%fused_computation | convolution fusion | flops 17187733504 | bytes 36182016 | tf_op jit(solution)/shard_map/dot_general | solution.py:40
  237.7 6.6 %copy.14 = f32[512,2,1536]{0,2,1:T(8,128)} copy(f32[512,2,1536]{2,0,1:T(8,128)} %multiply_reduce_fusion) | data formatting | bytes 12582912 | tf_op jit(solution)/shard_map/reduce_sum | solution.py:43
  244.2 2.2 dynamic-slice_bitcast_fusion
  246.4 1.5 collective-permute-start.1
  247.9 5.4 %collective-permute-done.1 = f32[2,512,768]{1,2,0:T(8,128)} collective-permute-done((f32[2,512,768]{1,2,0:T(8,128)S(1)}, f32[2,512,768]{1,2,0:T(8,128)}, u32[]{:S(2)}, u32[]{:S(2)}) %collective-permute-start.1) | collective-permute-done | bytes 3145760 | tf_op jit(solution)/shard_map/ppermute | solution.py:19
  253.3 3.6 %bitcast_add_fusion = f32[2,512,768]{1,2,0:T(8,128)S(1)} fusion(f32[2,512,768]{1,2,0:T(8,128)} %collective-permute-done.1, f32[512,2,2,768]{0,3,2,1:T(8,128)} %bitcast.38, s32[]{:T(128)S(6)} %select_n.34), kind=kLoop, calls=%fused_computation.8 | loop fusion | flops 786432 | bytes 9437188 | tf_op jit(solution)/shard_map/add | solution.py:19
  256.9 0.3 constant_dynamic-slice_fusion.1
  257.3 1.6 copy.17
  258.9 1.2 collective-permute-start.2
  260.1 0.5 copy.16
  260.6 34.2 %collective-permute-done.2 = f32[512,768]{1,0:T(8,128)} collective-permute-done((f32[512,768]{1,0:T(8,128)}, f32[512,768]{1,0:T(8,128)}, u32[]{:S(2)}, u32[]{:S(2)}) %collective-permute-start.2) | collective-permute-done | bytes 1572896 | tf_op jit(solution)/shard_map/ppermute | solution.py:19
  294.8 2.6 fusion.8
  (1 shorter events, 0.0 us)
Async XLA Ops:
  6.5 13.8 %copy-start = (s32[8]{0:T(128)S(1)}, s32[8]{0:T(128)}, u32[]{:S(2)}) copy-start(s32[8]{0:T(128)} %param.7) | copy-start | bytes 100
  6.5 14.9 %copy-start.1 = (f32[1024]{0:T(1024)S(1)}, f32[1024]{0:T(1024)}, u32[]{:S(2)}) copy-start(f32[1024]{0:T(1024)} %param.9) | copy-start | bytes 12292
  6.5 201.4 %all-gather.2.cloned.1.call-start = ((), (), s32[]{:S(2)}) async-start(), calls=%async_computation | async-start | bytes 25952256 | tf_op jit(solution)/shard_map/all_gather | solution.py:28
  6.5 11.7 %collective-permute-start = (bf16[2,48,2048]{2,1,0:T(8,128)(2,1)}, bf16[2,48,2048]{2,1,0:T(8,128)(2,1)S(1)}, u32[]{:S(2)}, u32[]{:S(2)}) collective-permute-start(bf16[2,48,2048]{2,1,0:T(8,128)(2,1)} %param.6), channel_id=1, source_target_pairs={{0,128},{128,0},{1,129},{129,1},{2,130},{130,2},{3,131},{131,3},{4... | collective-permute-start | bytes 1179656 | tf_op jit(solution)/shard_map/ppermute | solution.py:23
  246.4 6.9 %collective-permute-start.1 = (f32[2,512,768]{1,2,0:T(8,128)S(1)}, f32[2,512,768]{1,2,0:T(8,128)}, u32[]{:S(2)}, u32[]{:S(2)}) collective-permute-start(f32[2,512,768]{1,2,0:T(8,128)S(1)} %dynamic-slice_bitcast_fusion), channel_id=1, source_target_pairs={{0,1},{1,0},{2,3},{3,2},{4,5},{5,4},{6,7},{7,6},{8,9},{9,8},{10,11... | collective-permute-start | bytes 9437192 | tf_op jit(solution)/shard_map/ppermute | solution.py:19
  258.9 35.9 %collective-permute-start.2 = (f32[512,768]{1,0:T(8,128)}, f32[512,768]{1,0:T(8,128)}, u32[]{:S(2)}, u32[]{:S(2)}) collective-permute-start(f32[512,768]{1,0:T(8,128)} %bitcast.39), channel_id=1, source_target_pairs={{0,2},{2,0},{1,3},{3,1},{4,6},{6,4},{5,7},{7,5},{8,10},{10,8},{9,1... | collective-permute-start | bytes 4718600 | tf_op jit(solution)/shard_map/ppermute | solution.py:19
Sparse Core Ops, SparseCore 0:
  20.4 187.4 all-gather.1

commit v4 on v3

--- a/solution.py
+++ b/solution.py
@@ -10,13 +10,6 @@
 TOK = ("xh", "z", "y")
 FFN = ("xl", "c")
 SWAP = [(0, 1), (1, 0)]
-
-
-def halve(terms, axis, name):
-    own = lax.axis_index(name)
-    keep = lax.dynamic_index_in_dim(terms, own, axis=axis, keepdims=False)
-    send = lax.dynamic_index_in_dim(terms, 1 - own, axis=axis, keepdims=False)
-    return keep + lax.ppermute(send, name, perm=SWAP)
 
 
 def local(hidden, down_weight, block_expert, slot_token, slot_weight):
@@ -37,13 +30,23 @@
         pick.astype(hidden.dtype), hidden, (((2,), (0,)), ((), ())),
         preferred_element_type=jnp.float32,
     ).astype(hidden.dtype)
-    out = lax.dot_general(
-        rows, w_full, (((2,), (3,)), ((0,), (1,))), preferred_element_type=jnp.float32
-    )
-    token_terms = jnp.sum(scale[:, :, None, None] * out, axis=0)
-    half = token_terms.shape[2]
-    token_terms = token_terms.reshape(TOK_DEV, 2, 2, half // 2).transpose(1, 2, 0, 3)
-    mixed = halve(halve(token_terms, 1, "c"), 0, "xl")
+    rows, scale = lax.optimization_barrier((rows, scale))
+    quarter = w_full.shape[2] // 2
+    xl, c = lax.axis_index("xl"), lax.axis_index("c")
+
+    def terms(h, part):
+        w_part = lax.dynamic_slice_in_dim(w_full[h], part * quarter, quarter, axis=1)
+        out = lax.dot_general(
+            rows, w_part, (((2,), (2,)), ((0,), (0,))), preferred_element_type=jnp.float32
+        )
+        return jnp.sum(scale[:, :, None] * out, axis=0)
+
+    def by_core(h):
+        sent = lax.ppermute(terms(h, 1 - c), "c", perm=SWAP)
+        return terms(h, c) + sent
+
+    far = lax.ppermute(by_core(1 - xl), "xl", perm=SWAP)
+    mixed = by_core(xl) + far
     return mixed.astype(jnp.bfloat16)
 
 

time: 304 us -> 276 us (0.908)
  waiting for transfers between devices: 233 us -> 213 us
  local copies, waits for them, and re-layouts: 11.3 us -> 0.08 us
  matrix products: 29.8 us -> 36.5 us
  other arithmetic: 10 us -> 5.16 us
    ppermute x2 -> x3, waiting for transfers between devices: 39.7 us -> 27.8 us  [the longest x1 27.8 us: local(): far = lax.ppermute(by_core(1 - xl), 'xl', perm=SWAP)]
    all_gather x1, waiting for transfers between devices: 186 us -> 177 us  [local(): w_full = lax.all_gather(pair, ('z', 'y'), axis=2, tiled=True)]
    dot_general x1 -> x5, matrix products: 29.8 us -> 36.5 us  [the longest x4 28.3 us: terms(): lax.dot_general(rows, w_part, (((2,), (2,)), ((0,), (0,))), preferred_ele...]
    reduce_sum x1 -> x0, local copies, waits for them, and re-layouts: 6.57 us -> none  [local(): token_terms = jnp.sum(scale[:, :, None, None] * out, axis=0)]
    add x1, other arithmetic: 3.59 us -> 0.21 us  [by_core(): return terms(h, c) + sent]
  transfers between devices with their start and end apart: 4 -> 5, of which waited for: 4 -> 3; matrix products, arithmetic and copies ran while one was open for 1% -> 11% of each run, Pallas kernels for 0% -> 0%
where the time goes in v4:
time: 276 us; the launch traced here: 275 us
  waiting for transfers between devices  213 us (77%)
  matrix products  36.5 us (13%)
  between operations  13.5 us (5%)
  starting transfers between devices  6.64 us (2%)
  other arithmetic  5.16 us (2%)
    all_gather x1, waiting for transfers between devices, local(): w_full = lax.all_gather(pair, ('z', 'y'), axis=2, tiled=True)  177 us
    dot_general x4, matrix products, terms(): lax.dot_general(rows, w_part, (((2,), (2,)), ((0,), (0,))), preferred_ele...  28.3 us
    ppermute x1, waiting for transfers between devices, local(): far = lax.ppermute(by_core(1 - xl), 'xl', perm=SWAP)  27.8 us
    dot_general x1, matrix products, local(): lax.dot_general(pick.astype(hidden.dtype), hidden, (((2,), (0,)), ((), ()...  8.19 us
    ppermute x1, waiting for transfers between devices, local(): partner = lax.ppermute(down_weight, 'xh', perm=SWAP)  8.11 us
  transfers between devices with their start and end apart: 5, of which 3 were waited for; matrix products, arithmetic and copies ran while one was open for 11% of the time, Pallas kernels for 0%

profile of v4, /device:TPU:1, one launch (start us, length us, event | category | flops | bytes accessed | tf_op | source)
XLA Modules:
  0.0 275.3 jit_solution(11410379165173259799)
XLA Ops:
  6.5 0.0 copy-start
  6.5 0.0 copy-start.1
  6.5 0.0 all-gather.2.cloned.1.call-start
  6.5 3.6 %collective-permute-start = (bf16[2,48,2048]{2,1,0:T(8,128)(2,1)}, bf16[2,48,2048]{2,1,0:T(8,128)(2,1)S(1)}, u32[]{:S(2)}, u32[]{:S(2)}) collective-permute-start(bf16[2,48,2048]{2,1,0:T(8,128)(2,1)} %param.6), channel_id=1, source_target_pairs={{0,128},{128,0},{1,129},{129,1},{2,130},{130,2},{3,131},{131,3},{4... | collective-permute-start | bytes 1179656 | tf_op jit(solution)/shard_map/ppermute | solution.py:16
  10.1 8.1 %collective-permute-done = bf16[2,48,2048]{2,1,0:T(8,128)(2,1)S(1)} collective-permute-done((bf16[2,48,2048]{2,1,0:T(8,128)(2,1)}, bf16[2,48,2048]{2,1,0:T(8,128)(2,1)S(1)}, u32[]{:S(2)}, u32[]{:S(2)}) %collective-permute-start) | collective-permute-done | bytes 393248 | tf_op jit(solution)/shard_map/ppermute | solution.py:16
  18.2 1.1 select_bitcast_fusion.1
  19.3 0.9 pad_maximum_fusion
  20.2 0.0 all-gather.2.cloned.1.call-update
  20.3 0.0 copy-done
  20.3 0.1 broadcast_bitcast_fusion
  20.4 1.0 iota_compare_fusion
  21.4 0.0 copy-done.1
  21.4 0.8 fusion.14
  22.2 8.2 %fusion.16 = bf16[2,512,2048]{2,1,0:T(8,128)(2,1)} fusion(bf16[1024,2048]{1,0:T(8,128)(2,1)} %param.5, pred[2,1024]{1,0:T(4,128)(4,1)S(1)} %iota_compare_fusion.1, pred[512,1024]{1,0:T(8,128)(4,1)S(1)} %iota_compare_fusion), kind=kOutput, calls=%fused_computation.17 | convolution fusion | flops 4298113024 | bytes 8914944 | tf_op jit(solution)/shard_map/dot_general | solution.py:29
  30.4 177.5 %all-gather.2.cloned.1.call-done = bf16[2,2,1536,2048]{3,2,1,0:T(8,128)(2,1)} async-done(((bf16[2,2,48,2048]{3,2,1,0:T(8,128)(2,1)}), bf16[2,2,1536,2048]{3,2,1,0:T(8,128)(2,1)}) %all-gather.2.cloned.1.call-update) | async-done | bytes 25165840 | tf_op jit(solution)/shard_map/all_gather | solution.py:21
  207.9 7.7 %multiply_reduce_fusion = f32[512,768]{1,0:T(8,128)S(1)} fusion(f32[2,512]{1,0:T(2,128)S(1)} %fusion.14, bf16[2,512,2048]{2,1,0:T(8,128)(2,1)} %fusion.16, bf16[2,2,1536,2048]{3,2,1,0:T(8,128)(2,1)} %all-gather.2.cloned.1.call-done, s32[]{:T(128)S(6)} %select_n.51, s32[]{:T(128)S(6)} %select_n.49), kind=kOutput, calls=%fused_computation.18 | convolution fusion | flops 3222405120 | bytes 12062728 | tf_op jit(solution)/shard_map/dot_general | solution.py:39
  215.6 1.5 collective-permute-start.2
  217.1 0.0 copy-start.2
  217.1 7.8 %multiply_reduce_fusion.2 = f32[512,768]{1,0:T(8,128)S(1)} fusion(f32[2,512]{1,0:T(2,128)S(1)} %fusion.14, bf16[2,512,2048]{2,1,0:T(8,128)(2,1)} %fusion.16, bf16[2,2,1536,2048]{3,2,1,0:T(8,128)(2,1)} %all-gather.2.cloned.1.call-done, s32[]{:T(128)S(6)} %select_n.45, s32[]{:T(128)S(6)} %select_n.49), kind=kOutput, calls=%fused_computation.20 | convolution fusion | flops 3222405120 | bytes 12062728 | tf_op jit(solution)/shard_map/dot_general | solution.py:39
  224.9 0.3 collective-permute-start.1
  225.2 0.0 copy-done.2
  225.2 6.4 %multiply_reduce_fusion.1 = f32[512,768]{1,0:T(8,128)S(1)} fusion(f32[2,512]{1,0:T(2,128)S(1)} %fusion.14, bf16[2,512,2048]{2,1,0:T(8,128)(2,1)S(1)} %copy-done.2, bf16[2,2,1536,2048]{3,2,1,0:T(8,128)(2,1)} %all-gather.2.cloned.1.call-done, s32[]{:T(128)S(6)} %select_n.51, s32[]{:T(128)S(6)} %select_n.47), kind=kOutput, calls=%fused_computation.19 | convolution fusion | flops 3222405120 | bytes 12062728 | tf_op jit(solution)/shard_map/dot_general | solution.py:39
  231.6 0.0 collective-permute-done.2
  231.6 0.2 add.47
  231.8 1.3 collective-permute-start.3
  233.1 6.4 %multiply_reduce_fusion.3 = f32[512,768]{1,0:T(8,128)S(1)} fusion(f32[2,512]{1,0:T(2,128)S(1)} %fusion.14, bf16[2,512,2048]{2,1,0:T(8,128)(2,1)S(1)} %copy-done.2, bf16[2,2,1536,2048]{3,2,1,0:T(8,128)(2,1)} %all-gather.2.cloned.1.call-done, s32[]{:T(128)S(6)} %select_n.45, s32[]{:T(128)S(6)} %select_n.47), kind=kOutput, calls=%fused_computation.21 | convolution fusion | flops 3222405120 | bytes 12062728 | tf_op jit(solution)/shard_map/dot_general | solution.py:39
  239.5 0.0 collective-permute-done.1
  239.5 27.8 %collective-permute-done.3 = f32[512,768]{1,0:T(8,128)S(1)} collective-permute-done((f32[512,768]{1,0:T(8,128)S(1)}, f32[512,768]{1,0:T(8,128)S(1)}, u32[]{:S(2)}, u32[]{:S(2)}) %collective-permute-start.3) | collective-permute-done | bytes 1572896 | tf_op jit(solution)/shard_map/ppermute | solution.py:48
  267.3 1.1 add_convert_fusion
  (1 shorter events, 0.0 us)
Async XLA Ops:
  6.5 13.7 %copy-start = (s32[8]{0:T(128)S(1)}, s32[8]{0:T(128)}, u32[]{:S(2)}) copy-start(s32[8]{0:T(128)} %param.7) | copy-start | bytes 100
  6.5 14.8 %copy-start.1 = (f32[1024]{0:T(1024)S(1)}, f32[1024]{0:T(1024)}, u32[]{:S(2)}) copy-start(f32[1024]{0:T(1024)} %param.9) | copy-start | bytes 12292
  6.5 201.3 %all-gather.2.cloned.1.call-start = ((), (), s32[]{:S(2)}) async-start(), calls=%async_computation | async-start | bytes 25952256 | tf_op jit(solution)/shard_map/all_gather | solution.py:21
  6.5 11.7 %collective-permute-start = (bf16[2,48,2048]{2,1,0:T(8,128)(2,1)}, bf16[2,48,2048]{2,1,0:T(8,128)(2,1)S(1)}, u32[]{:S(2)}, u32[]{:S(2)}) collective-permute-start(bf16[2,48,2048]{2,1,0:T(8,128)(2,1)} %param.6), channel_id=1, source_target_pairs={{0,128},{128,0},{1,129},{129,1},{2,130},{130,2},{3,131},{131,3},{4... | collective-permute-start | bytes 1179656 | tf_op jit(solution)/shard_map/ppermute | solution.py:16
  215.6 16.0 %collective-permute-start.2 = (f32[512,768]{1,0:T(8,128)S(1)}, f32[512,768]{1,0:T(8,128)S(1)}, u32[]{:S(2)}, u32[]{:S(2)}) collective-permute-start(f32[512,768]{1,0:T(8,128)S(1)} %multiply_reduce_fusion), channel_id=1, source_target_pairs={{0,1},{1,0},{2,3},{3,2},{4,5},{5,4},{6,7},{7,6},{8,9},{9,8},{10,11... | collective-permute-start | bytes 4718600 | tf_op jit(solution)/shard_map/ppermute | solution.py:45
  217.1 8.1 %copy-start.2 = (bf16[2,512,2048]{2,1,0:T(8,128)(2,1)S(1)}, bf16[2,512,2048]{2,1,0:T(8,128)(2,1)}, u32[]{:S(2)}) copy-start(bf16[2,512,2048]{2,1,0:T(8,128)(2,1)} %fusion.16) | copy-start | bytes 12582916
  224.9 14.6 %collective-permute-start.1 = (f32[512,768]{1,0:T(8,128)S(1)}, f32[512,768]{1,0:T(8,128)S(1)}, u32[]{:S(2)}, u32[]{:S(2)}) collective-permute-start(f32[512,768]{1,0:T(8,128)S(1)} %multiply_reduce_fusion.2), channel_id=1, source_target_pairs={{0,1},{1,0},{2,3},{3,2},{4,5},{5,4},{6,7},{7,6},{8,9},{9,8},{10,11... | collective-permute-start | bytes 4718600 | tf_op jit(solution)/shard_map/ppermute | solution.py:45
  231.8 35.5 %collective-permute-start.3 = (f32[512,768]{1,0:T(8,128)S(1)}, f32[512,768]{1,0:T(8,128)S(1)}, u32[]{:S(2)}, u32[]{:S(2)}) collective-permute-start(f32[512,768]{1,0:T(8,128)S(1)} %add.47), channel_id=1, source_target_pairs={{0,2},{2,0},{1,3},{3,1},{4,6},{6,4},{5,7},{7,5},{8,10},{10,8},{9,1... | collective-permute-start | bytes 4718600 | tf_op jit(solution)/shard_map/ppermute | solution.py:48
Sparse Core Ops, SparseCore 0:
  20.4 187.4 all-gather.1

commit v5 on v4

--- a/solution.py
+++ b/solution.py
@@ -3,16 +3,18 @@
 from jax import lax
 from jax.sharding import Mesh, PartitionSpec as P
 
+
 EXP = 2
 BLOCK = 128
 TOK_DEV = 512
+CHUNKS = 2
 
 TOK = ("xh", "z", "y")
 FFN = ("xl", "c")
 SWAP = [(0, 1), (1, 0)]
 
 
-def local(hidden, down_weight, block_expert, slot_token, slot_weight):
+def body(hidden, down_weight, block_expert, slot_token, slot_weight):
     partner = lax.ppermute(down_weight, "xh", perm=SWAP)
     first = lax.axis_index("xh") == 0
     pair = jnp.stack(
@@ -34,19 +36,26 @@
     quarter = w_full.shape[2] // 2
     xl, c = lax.axis_index("xl"), lax.axis_index("c")
 
-    def terms(h, part):
+    def terms(rows, scale, h, part):
         w_part = lax.dynamic_slice_in_dim(w_full[h], part * quarter, quarter, axis=1)
         out = lax.dot_general(
             rows, w_part, (((2,), (2,)), ((0,), (0,))), preferred_element_type=jnp.float32
         )
         return jnp.sum(scale[:, :, None] * out, axis=0)
 
-    def by_core(h):
-        sent = lax.ppermute(terms(h, 1 - c), "c", perm=SWAP)
-        return terms(h, c) + sent
+    def by_core(rows, scale, h):
+        sent = lax.ppermute(terms(rows, scale, h, 1 - c), "c", perm=SWAP)
+        return terms(rows, scale, h, c) + sent
 
-    far = lax.ppermute(by_core(1 - xl), "xl", perm=SWAP)
-    mixed = by_core(xl) + far
+    chunk = TOK_DEV // CHUNKS
+    far = []
+    for k in range(CHUNKS):
+        part = slice(k * chunk, (k + 1) * chunk)
+        far.append(by_core(rows[:, part], scale[:, part], 1 - xl))
+    near_rows, near_scale, *far = lax.optimization_barrier((rows, scale, *far))
+    far = [lax.ppermute(piece, "xl", perm=SWAP) for piece in far]
+    near = by_core(near_rows, near_scale, xl)
+    mixed = near + jnp.concatenate(far, axis=0)
     return mixed.astype(jnp.bfloat16)
 
 
@@ -54,6 +63,4 @@
     tok_size, ffn_size = mesh.devices.shape
     fine = Mesh(mesh.devices.reshape(2, tok_size // 8, 4, 2, ffn_size // 2), TOK + FFN)
     placed = (P(TOK, FFN), P(None, TOK, FFN), P(TOK), P(TOK), P(TOK))
-    return jax.shard_map(
-        local, mesh=fine, in_specs=placed, out_specs=P(TOK, FFN), check_vma=False
-    )
+    return jax.shard_map(body, mesh=fine, in_specs=placed, out_specs=P(TOK, FFN), check_vma=False)

time: 276 us -> 281 us (1.018)
  matrix products: 36.5 us -> 40.8 us
    dot_general x4 -> x6, matrix products: 28.3 us -> 32.6 us  [terms(): lax.dot_general(rows, w_part, (((2,), (2,)), ((0,), (0,))), preferred_ele...]
    ppermute x4 -> x6, starting transfers between devices: 6.64 us -> 7.37 us  [the longest x1 3.56 us: body(): partner = lax.ppermute(down_weight, 'xh', perm=SWAP)]
    ppermute x4 -> x6, waiting for transfers between devices: 35.9 us -> 36.1 us  [the longest x2 28 us: body(): far = [lax.ppermute(piece, 'xl', perm=SWAP) for piece in far]]
  transfers between devices with their start and end apart: 5 -> 7, of which waited for: 3 -> 4; matrix products, arithmetic and copies ran while one was open for 11% -> 11% of each run, Pallas kernels for 0% -> 0%
where the time goes in v5:
time: 281 us; the launch traced here: 280 us
  waiting for transfers between devices  214 us (76%)
  matrix products  40.8 us (15%)
  between operations  13.5 us (5%)
  starting transfers between devices  7.37 us (3%)
  other arithmetic  5.12 us (2%)
    all_gather x1, waiting for transfers between devices, body(): w_full = lax.all_gather(pair, ('z', 'y'), axis=2, tiled=True)  177 us
    dot_general x6, matrix products, terms(): lax.dot_general(rows, w_part, (((2,), (2,)), ((0,), (0,))), preferred_ele...  32.6 us
    ppermute x2, waiting for transfers between devices, body(): far = [lax.ppermute(piece, 'xl', perm=SWAP) for piece in far]  28 us
    dot_general x1, matrix products, body(): lax.dot_general(pick.astype(hidden.dtype), hidden, (((2,), (0,)), ((), ()...  8.19 us
    ppermute x1, waiting for transfers between devices, body(): partner = lax.ppermute(down_weight, 'xh', perm=SWAP)  8.11 us
  transfers between devices with their start and end apart: 7, of which 4 were waited for; matrix products, arithmetic and copies ran while one was open for 11% of the time, Pallas kernels for 0%

profile of v5, /device:TPU:1, one launch (start us, length us, event | category | flops | bytes accessed | tf_op | source)
XLA Modules:
  0.0 280.5 jit_solution(6341830621298594309)
XLA Ops:
  6.5 0.0 copy-start
  6.5 0.0 copy-start.1
  6.5 0.0 all-gather.2.cloned.1.call-start
  6.5 3.6 %collective-permute-start = (bf16[2,48,2048]{2,1,0:T(8,128)(2,1)}, bf16[2,48,2048]{2,1,0:T(8,128)(2,1)S(1)}, u32[]{:S(2)}, u32[]{:S(2)}) collective-permute-start(bf16[2,48,2048]{2,1,0:T(8,128)(2,1)} %param.6), channel_id=1, source_target_pairs={{0,128},{128,0},{1,129},{129,1},{2,130},{130,2},{3,131},{131,3},{4... | collective-permute-start | bytes 1179656 | tf_op jit(solution)/shard_map/ppermute | solution.py:18
  10.1 8.1 %collective-permute-done = bf16[2,48,2048]{2,1,0:T(8,128)(2,1)S(1)} collective-permute-done((bf16[2,48,2048]{2,1,0:T(8,128)(2,1)}, bf16[2,48,2048]{2,1,0:T(8,128)(2,1)S(1)}, u32[]{:S(2)}, u32[]{:S(2)}) %collective-permute-start) | collective-permute-done | bytes 393248 | tf_op jit(solution)/shard_map/ppermute | solution.py:18
  18.2 1.1 select_bitcast_fusion.1
  19.3 0.9 pad_maximum_fusion
  20.2 0.0 all-gather.2.cloned.1.call-update
  20.3 0.0 copy-done
  20.3 0.1 broadcast_bitcast_fusion
  20.4 1.0 iota_compare_fusion
  21.4 0.0 copy-done.1
  21.4 0.8 fusion.20
  22.2 8.2 %fusion.22 = bf16[2,512,2048]{2,1,0:T(8,128)(2,1)} fusion(bf16[1024,2048]{1,0:T(8,128)(2,1)} %param.5, pred[2,1024]{1,0:T(4,128)(4,1)S(1)} %iota_compare_fusion.1, pred[512,1024]{1,0:T(8,128)(4,1)S(1)} %iota_compare_fusion), kind=kOutput, calls=%fused_computation.23 | convolution fusion | flops 4298113024 | bytes 8914944 | tf_op jit(solution)/shard_map/dot_general | solution.py:31
  30.4 177.5 %all-gather.2.cloned.1.call-done = bf16[2,2,1536,2048]{3,2,1,0:T(8,128)(2,1)} async-done(((bf16[2,2,48,2048]{3,2,1,0:T(8,128)(2,1)}), bf16[2,2,1536,2048]{3,2,1,0:T(8,128)(2,1)}) %all-gather.2.cloned.1.call-update) | async-done | bytes 25165840 | tf_op jit(solution)/shard_map/all_gather | solution.py:23
  207.9 0.0 copy-start.2
  207.9 5.5 %multiply_reduce_fusion.4 = f32[256,768]{1,0:T(8,128)S(1)} fusion(bf16[2,2,1536,2048]{3,2,1,0:T(8,128)(2,1)} %all-gather.2.cloned.1.call-done, s32[]{:T(128)S(6)} %select_n.49, s32[]{:T(128)S(6)} %select_n.53, bf16[2,512,2048]{2,1,0:T(8,128)(2,1)} %fusion.22, f32[2,256]{1,0:T(2,128)S(1)} %get-tuple-element.20), kind=kOutput, calls=%fused_computation.37 | convolution fusion | flops 1611202560 | bytes 9177096 | tf_op jit(solution)/shard_map/dot_general | solution.py:41
  213.4 1.5 collective-permute-start.1
  214.9 0.0 copy-done.2
  214.9 4.8 %multiply_reduce_fusion.2 = f32[256,768]{1,0:T(8,128)S(1)} fusion(bf16[2,2,1536,2048]{3,2,1,0:T(8,128)(2,1)} %all-gather.2.cloned.1.call-done, s32[]{:T(128)S(6)} %select_n.49, s32[]{:T(128)S(6)} %select_n.53, bf16[2,512,2048]{2,1,0:T(8,128)(2,1)S(1)} %copy-done.2, f32[2,256]{1,0:T(2,128)S(1)} %get-tuple-element.19), kind=kOutput, calls=%fused_computation.35 | convolution fusion | flops 1611202560 | bytes 9177096 | tf_op jit(solution)/shard_map/dot_general | solution.py:41
  219.7 0.3 collective-permute-start.2
  220.0 4.7 %multiply_reduce_fusion.3 = f32[256,768]{1,0:T(8,128)S(1)} fusion(bf16[2,2,1536,2048]{3,2,1,0:T(8,128)(2,1)} %all-gather.2.cloned.1.call-done, s32[]{:T(128)S(6)} %select_n.49, s32[]{:T(128)S(6)} %select_n.51, bf16[2,512,2048]{2,1,0:T(8,128)(2,1)S(1)} %copy-done.2, f32[2,256]{1,0:T(2,128)S(1)} %get-tuple-element.19), kind=kOutput, calls=%fused_computation.36 | convolution fusion | flops 1611202560 | bytes 9177096 | tf_op jit(solution)/shard_map/dot_general | solution.py:41
  224.7 4.8 %multiply_reduce_fusion.5 = f32[256,768]{1,0:T(8,128)S(1)} fusion(bf16[2,2,1536,2048]{3,2,1,0:T(8,128)(2,1)} %all-gather.2.cloned.1.call-done, s32[]{:T(128)S(6)} %select_n.49, s32[]{:T(128)S(6)} %select_n.51, bf16[2,512,2048]{2,1,0:T(8,128)(2,1)S(1)} %copy-done.2, f32[2,256]{1,0:T(2,128)S(1)} %get-tuple-element.20), kind=kOutput, calls=%fused_computation.38 | convolution fusion | flops 1611202560 | bytes 9177096 | tf_op jit(solution)/shard_map/dot_general | solution.py:41
  229.5 0.0 collective-permute-done.1
  229.5 0.1 add.52
  229.6 0.0 collective-permute-done.2
  229.6 0.1 add.53
  229.7 6.4 %multiply_reduce_fusion = f32[512,768]{1,0:T(8,128)S(1)} fusion(f32[2,512]{1,0:T(2,128)S(1)} %fusion.20, bf16[2,512,2048]{2,1,0:T(8,128)(2,1)S(1)} %copy-done.2, bf16[2,2,1536,2048]{3,2,1,0:T(8,128)(2,1)} %all-gather.2.cloned.1.call-done, s32[]{:T(128)S(6)} %select_n.55, s32[]{:T(128)S(6)} %select_n.53), kind=kOutput, calls=%fused_computation.24 | convolution fusion | flops 3222405120 | bytes 12062728 | tf_op jit(solution)/shard_map/dot_general | solution.py:41
  236.1 0.6 collective-permute-start.3
  236.7 1.2 collective-permute-start.4
  237.9 0.3 collective-permute-start.5
  238.1 6.4 %multiply_reduce_fusion.1 = f32[512,768]{1,0:T(8,128)S(1)} fusion(f32[2,512]{1,0:T(2,128)S(1)} %fusion.20, bf16[2,512,2048]{2,1,0:T(8,128)(2,1)S(1)} %copy-done.2, bf16[2,2,1536,2048]{3,2,1,0:T(8,128)(2,1)} %all-gather.2.cloned.1.call-done, s32[]{:T(128)S(6)} %select_n.55, s32[]{:T(128)S(6)} %select_n.51), kind=kOutput, calls=%fused_computation.25 | convolution fusion | flops 3222405120 | bytes 12062728 | tf_op jit(solution)/shard_map/dot_general | solution.py:41
  244.5 11.1 %collective-permute-done.4 = f32[256,768]{1,0:T(8,128)S(1)} collective-permute-done((f32[256,768]{1,0:T(8,128)S(1)}, f32[256,768]{1,0:T(8,128)S(1)}, u32[]{:S(2)}, u32[]{:S(2)}) %collective-permute-start.4) | collective-permute-done | bytes 786464 | tf_op jit(solution)/shard_map/ppermute | solution.py:56
  255.7 16.9 %collective-permute-done.5 = f32[256,768]{1,0:T(8,128)S(1)} collective-permute-done((f32[256,768]{1,0:T(8,128)S(1)}, f32[256,768]{1,0:T(8,128)S(1)}, u32[]{:S(2)}, u32[]{:S(2)}) %collective-permute-start.5) | collective-permute-done | bytes 786464 | tf_op jit(solution)/shard_map/ppermute | solution.py:56
  272.5 0.0 collective-permute-done.3
  272.5 1.1 fusion.33
  (2 shorter events, 0.0 us)
Async XLA Ops:
  6.5 13.7 %copy-start = (s32[8]{0:T(128)S(1)}, s32[8]{0:T(128)}, u32[]{:S(2)}) copy-start(s32[8]{0:T(128)} %param.7) | copy-start | bytes 100
  6.5 14.8 %copy-start.1 = (f32[1024]{0:T(1024)S(1)}, f32[1024]{0:T(1024)}, u32[]{:S(2)}) copy-start(f32[1024]{0:T(1024)} %param.9) | copy-start | bytes 12292
  6.5 201.3 %all-gather.2.cloned.1.call-start = ((), (), s32[]{:S(2)}) async-start(), calls=%async_computation | async-start | bytes 25952256 | tf_op jit(solution)/shard_map/all_gather | solution.py:23
  6.5 11.7 %collective-permute-start = (bf16[2,48,2048]{2,1,0:T(8,128)(2,1)}, bf16[2,48,2048]{2,1,0:T(8,128)(2,1)S(1)}, u32[]{:S(2)}, u32[]{:S(2)}) collective-permute-start(bf16[2,48,2048]{2,1,0:T(8,128)(2,1)} %param.6), channel_id=1, source_target_pairs={{0,128},{128,0},{1,129},{129,1},{2,130},{130,2},{3,131},{131,3},{4... | collective-permute-start | bytes 1179656 | tf_op jit(solution)/shard_map/ppermute | solution.py:18
  207.9 7.0 %copy-start.2 = (bf16[2,512,2048]{2,1,0:T(8,128)(2,1)S(1)}, bf16[2,512,2048]{2,1,0:T(8,128)(2,1)}, u32[]{:S(2)}) copy-start(bf16[2,512,2048]{2,1,0:T(8,128)(2,1)} %fusion.22) | copy-start | bytes 12582916
  213.4 16.0 %collective-permute-start.1 = (f32[256,768]{1,0:T(8,128)S(1)}, f32[256,768]{1,0:T(8,128)S(1)}, u32[]{:S(2)}, u32[]{:S(2)}) collective-permute-start(f32[256,768]{1,0:T(8,128)S(1)} %multiply_reduce_fusion.4), channel_id=1, source_target_pairs={{0,1},{1,0},{2,3},{3,2},{4,5},{5,4},{6,7},{7,6},{8,9},{9,8},{10,11... | collective-permute-start | bytes 2359304 | tf_op jit(solution)/shard_map/ppermute | solution.py:47
  219.7 9.9 %collective-permute-start.2 = (f32[256,768]{1,0:T(8,128)S(1)}, f32[256,768]{1,0:T(8,128)S(1)}, u32[]{:S(2)}, u32[]{:S(2)}) collective-permute-start(f32[256,768]{1,0:T(8,128)S(1)} %multiply_reduce_fusion.2), channel_id=1, source_target_pairs={{0,1},{1,0},{2,3},{3,2},{4,5},{5,4},{6,7},{7,6},{8,9},{9,8},{10,11... | collective-permute-start | bytes 2359304 | tf_op jit(solution)/shard_map/ppermute | solution.py:47
  236.1 36.4 %collective-permute-start.3 = (f32[512,768]{1,0:T(8,128)S(1)}, f32[512,768]{1,0:T(8,128)S(1)}, u32[]{:S(2)}, u32[]{:S(2)}) collective-permute-start(f32[512,768]{1,0:T(8,128)S(1)} %multiply_reduce_fusion), channel_id=1, source_target_pairs={{0,1},{1,0},{2,3},{3,2},{4,5},{5,4},{6,7},{7,6},{8,9},{9,8},{10,11... | collective-permute-start | bytes 4718600 | tf_op jit(solution)/shard_map/ppermute | solution.py:47
  236.7 19.0 %collective-permute-start.4 = (f32[256,768]{1,0:T(8,128)S(1)}, f32[256,768]{1,0:T(8,128)S(1)}, u32[]{:S(2)}, u32[]{:S(2)}) collective-permute-start(f32[256,768]{1,0:T(8,128)S(1)} %add.52), channel_id=1, source_target_pairs={{0,2},{2,0},{1,3},{3,1},{4,6},{6,4},{5,7},{7,5},{8,10},{10,8},{9,1... | collective-permute-start | bytes 2359304 | tf_op jit(solution)/shard_map/ppermute | solution.py:56
  237.9 34.7 %collective-permute-start.5 = (f32[256,768]{1,0:T(8,128)S(1)}, f32[256,768]{1,0:T(8,128)S(1)}, u32[]{:S(2)}, u32[]{:S(2)}) collective-permute-start(f32[256,768]{1,0:T(8,128)S(1)} %add.53), channel_id=1, source_target_pairs={{0,2},{2,0},{1,3},{3,1},{4,6},{6,4},{5,7},{7,5},{8,10},{10,8},{9,1... | collective-permute-start | bytes 2359304 | tf_op jit(solution)/shard_map/ppermute | solution.py:56
Sparse Core Ops, SparseCore 0:
  20.4 187.4 all-gather.1

commit v6 on v5

--- a/solution.py
+++ b/solution.py
@@ -7,7 +7,6 @@
 EXP = 2
 BLOCK = 128
 TOK_DEV = 512
-CHUNKS = 2
 
 TOK = ("xh", "z", "y")
 FFN = ("xl", "c")
@@ -16,11 +15,9 @@
 
 def body(hidden, down_weight, block_expert, slot_token, slot_weight):
     partner = lax.ppermute(down_weight, "xh", perm=SWAP)
-    first = lax.axis_index("xh") == 0
-    pair = jnp.stack(
-        [jnp.where(first, down_weight, partner), jnp.where(first, partner, down_weight)], axis=0
-    )
+    pair = jnp.stack([down_weight, partner], axis=0)
     w_full = lax.all_gather(pair, ("z", "y"), axis=2, tiled=True)
+    xh = lax.axis_index("xh")
     slot_expert = jnp.repeat(block_expert, BLOCK)
     tokens = jnp.arange(TOK_DEV, dtype=jnp.int32)
     experts = jnp.arange(EXP, dtype=jnp.int32)
@@ -37,7 +34,7 @@
     xl, c = lax.axis_index("xl"), lax.axis_index("c")
 
     def terms(rows, scale, h, part):
-        w_part = lax.dynamic_slice_in_dim(w_full[h], part * quarter, quarter, axis=1)
+        w_part = lax.dynamic_slice_in_dim(w_full[(h + xh) % 2], part * quarter, quarter, axis=1)
         out = lax.dot_general(
             rows, w_part, (((2,), (2,)), ((0,), (0,))), preferred_element_type=jnp.float32
         )
@@ -47,15 +44,11 @@
         sent = lax.ppermute(terms(rows, scale, h, 1 - c), "c", perm=SWAP)
         return terms(rows, scale, h, c) + sent
 
-    chunk = TOK_DEV // CHUNKS
-    far = []
-    for k in range(CHUNKS):
-        part = slice(k * chunk, (k + 1) * chunk)
-        far.append(by_core(rows[:, part], scale[:, part], 1 - xl))
-    near_rows, near_scale, *far = lax.optimization_barrier((rows, scale, *far))
-    far = [lax.ppermute(piece, "xl", perm=SWAP) for piece in far]
+    far = by_core(rows, scale, 1 - xl)
+    near_rows, near_scale, far = lax.optimization_barrier((rows, scale, far))
+    far = lax.ppermute(far, "xl", perm=SWAP)
     near = by_core(near_rows, near_scale, xl)
-    mixed = near + jnp.concatenate(far, axis=0)
+    mixed = near + far
     return mixed.astype(jnp.bfloat16)
 
 

time: 281 us -> 278 us (0.989)
  matrix products: 40.8 us -> 36.6 us
    dot_general x6 -> x4, matrix products: 32.6 us -> 28.4 us  [terms(): lax.dot_general(rows, w_part, (((2,), (2,)), ((0,), (0,))), preferred_ele...]
    ppermute x2 -> x1, waiting for transfers between devices: 28 us -> 27.7 us  [body(): far = lax.ppermute(far, 'xl', perm=SWAP)]
  transfers between devices with their start and end apart: 7 -> 5, of which waited for: 4 -> 3; matrix products, arithmetic and copies ran while one was open for 11% -> 9% of each run, Pallas kernels for 0% -> 0%
where the time goes in v6:
time: 278 us; the launch traced here: 277 us
  waiting for transfers between devices  213 us (77%)
  matrix products  36.6 us (13%)
  between operations  13.5 us (5%)
  starting transfers between devices  6.69 us (2%)
  other arithmetic  5.79 us (2%)
    all_gather x1, waiting for transfers between devices, body(): w_full = lax.all_gather(pair, ('z', 'y'), axis=2, tiled=True)  177 us
    dot_general x4, matrix products, terms(): lax.dot_general(rows, w_part, (((2,), (2,)), ((0,), (0,))), preferred_ele...  28.4 us
    ppermute x1, waiting for transfers between devices, body(): far = lax.ppermute(far, 'xl', perm=SWAP)  27.7 us
    dot_general x1, matrix products, body(): lax.dot_general(pick.astype(hidden.dtype), hidden, (((2,), (0,)), ((), ()...  8.19 us
    ppermute x1, waiting for transfers between devices, body(): partner = lax.ppermute(down_weight, 'xh', perm=SWAP)  8.11 us
  transfers between devices with their start and end apart: 5, of which 3 were waited for; matrix products, arithmetic and copies ran while one was open for 9% of the time, Pallas kernels for 0%

profile of v6, /device:TPU:1, one launch (start us, length us, event | category | flops | bytes accessed | tf_op | source)
XLA Modules:
  0.0 277.3 jit_solution(9648971999477995501)
XLA Ops:
  6.5 0.0 copy-start
  6.5 0.0 all-gather.2.cloned.1.call-start
  6.5 3.6 %collective-permute-start = (bf16[2,48,2048]{2,1,0:T(8,128)(2,1)}, bf16[2,48,2048]{2,1,0:T(8,128)(2,1)S(1)}, u32[]{:S(2)}, u32[]{:S(2)}) collective-permute-start(bf16[2,48,2048]{2,1,0:T(8,128)(2,1)} %param.6), channel_id=1, source_target_pairs={{0,128},{128,0},{1,129},{129,1},{2,130},{130,2},{3,131},{131,3},{4... | collective-permute-start | bytes 1179656 | tf_op jit(solution)/shard_map/ppermute | solution.py:17
  10.1 8.1 %collective-permute-done = bf16[2,48,2048]{2,1,0:T(8,128)(2,1)S(1)} collective-permute-done((bf16[2,48,2048]{2,1,0:T(8,128)(2,1)}, bf16[2,48,2048]{2,1,0:T(8,128)(2,1)S(1)}, u32[]{:S(2)}, u32[]{:S(2)}) %collective-permute-start) | collective-permute-done | bytes 393248 | tf_op jit(solution)/shard_map/ppermute | solution.py:17
  18.2 1.9 pad_maximum_fusion
  20.2 0.0 all-gather.2.cloned.1.call-update
  20.2 0.0 copy-done
  20.2 0.1 broadcast_bitcast_fusion
  20.3 1.0 iota_compare_fusion
  21.3 1.5 fusion.14
  22.8 8.2 %fusion.16 = bf16[2,512,2048]{2,1,0:T(8,128)(2,1)} fusion(bf16[1024,2048]{1,0:T(8,128)(2,1)} %param.5, pred[2,1024]{1,0:T(4,128)(4,1)S(1)} %iota_compare_fusion.1, pred[512,1024]{1,0:T(8,128)(4,1)S(1)} %iota_compare_fusion), kind=kOutput, calls=%fused_computation.17 | convolution fusion | flops 4298113024 | bytes 8914944 | tf_op jit(solution)/shard_map/dot_general | solution.py:28
  31.0 176.8 %all-gather.2.cloned.1.call-done = bf16[2,2,1536,2048]{3,2,1,0:T(8,128)(2,1)} async-done(((bf16[2,2,48,2048]{3,2,1,0:T(8,128)(2,1)}), bf16[2,2,1536,2048]{3,2,1,0:T(8,128)(2,1)}) %all-gather.2.cloned.1.call-update) | async-done | bytes 25165840 | tf_op jit(solution)/shard_map/all_gather | solution.py:19
  207.8 7.7 %multiply_reduce_fusion.2 = f32[512,768]{1,0:T(8,128)S(1)} fusion(f32[2,512]{1,0:T(2,128)S(1)} %fusion.14, bf16[2,512,2048]{2,1,0:T(8,128)(2,1)} %fusion.16, bf16[2,2,1536,2048]{3,2,1,0:T(8,128)(2,1)} %all-gather.2.cloned.1.call-done, s32[]{:T(128)S(6)} %select_n.46, s32[]{:T(128)S(6)} %select_n.50), kind=kOutput, calls=%fused_computation.20 | convolution fusion | flops 3222405120 | bytes 12062728 | tf_op jit(solution)/shard_map/dot_general | solution.py:38
  215.5 1.6 collective-permute-start.1
  217.2 7.7 %multiply_reduce_fusion.3 = f32[512,768]{1,0:T(8,128)S(1)} fusion(f32[2,512]{1,0:T(2,128)S(1)} %fusion.14, bf16[2,512,2048]{2,1,0:T(8,128)(2,1)} %fusion.16, bf16[2,2,1536,2048]{3,2,1,0:T(8,128)(2,1)} %all-gather.2.cloned.1.call-done, s32[]{:T(128)S(6)} %select_n.46, s32[]{:T(128)S(6)} %select_n.48), kind=kOutput, calls=%fused_computation.21 | convolution fusion | flops 3222405120 | bytes 12062728 | tf_op jit(solution)/shard_map/dot_general | solution.py:38
  224.9 0.0 copy-start.1
  224.9 0.0 collective-permute-done.1
  224.9 0.2 add.63
  225.1 2.0 copy-done.1
  227.1 6.5 %multiply_reduce_fusion = f32[512,768]{1,0:T(8,128)S(1)} fusion(f32[2,512]{1,0:T(2,128)S(1)} %fusion.14, bf16[2,512,2048]{2,1,0:T(8,128)(2,1)S(1)} %copy-done.1, bf16[2,2,1536,2048]{3,2,1,0:T(8,128)(2,1)} %all-gather.2.cloned.1.call-done, s32[]{:T(128)S(6)} %select_n.53, s32[]{:T(128)S(6)} %select_n.50), kind=kOutput, calls=%fused_computation.18 | convolution fusion | flops 3222405120 | bytes 12062728 | tf_op jit(solution)/shard_map/dot_general | solution.py:38
  233.6 0.1 collective-permute-start.2
  233.7 1.3 collective-permute-start.3
  235.1 6.5 %multiply_reduce_fusion.1 = f32[512,768]{1,0:T(8,128)S(1)} fusion(f32[2,512]{1,0:T(2,128)S(1)} %fusion.14, bf16[2,512,2048]{2,1,0:T(8,128)(2,1)S(1)} %copy-done.1, bf16[2,2,1536,2048]{3,2,1,0:T(8,128)(2,1)} %all-gather.2.cloned.1.call-done, s32[]{:T(128)S(6)} %select_n.53, s32[]{:T(128)S(6)} %select_n.48), kind=kOutput, calls=%fused_computation.19 | convolution fusion | flops 3222405120 | bytes 12062728 | tf_op jit(solution)/shard_map/dot_general | solution.py:38
  241.6 0.0 collective-permute-done.2
  241.6 27.7 %collective-permute-done.3 = f32[512,768]{1,0:T(8,128)S(1)} collective-permute-done((f32[512,768]{1,0:T(8,128)S(1)}, f32[512,768]{1,0:T(8,128)S(1)}, u32[]{:S(2)}, u32[]{:S(2)}) %collective-permute-start.3) | collective-permute-done | bytes 1572896 | tf_op jit(solution)/shard_map/ppermute | solution.py:49
  269.3 1.1 add_convert_fusion
  (1 shorter events, 0.0 us)
Async XLA Ops:
  6.5 13.7 %copy-start = (s32[8]{0:T(128)S(1)}, s32[8]{0:T(128)}, u32[]{:S(2)}) copy-start(s32[8]{0:T(128)} %param.7) | copy-start | bytes 100
  6.5 201.3 %all-gather.2.cloned.1.call-start = ((), (), s32[]{:S(2)}) async-start(), calls=%async_computation | async-start | bytes 25952256 | tf_op jit(solution)/shard_map/all_gather | solution.py:19
  6.5 11.7 %collective-permute-start = (bf16[2,48,2048]{2,1,0:T(8,128)(2,1)}, bf16[2,48,2048]{2,1,0:T(8,128)(2,1)S(1)}, u32[]{:S(2)}, u32[]{:S(2)}) collective-permute-start(bf16[2,48,2048]{2,1,0:T(8,128)(2,1)} %param.6), channel_id=1, source_target_pairs={{0,128},{128,0},{1,129},{129,1},{2,130},{130,2},{3,131},{131,3},{4... | collective-permute-start | bytes 1179656 | tf_op jit(solution)/shard_map/ppermute | solution.py:17
  215.5 9.4 %collective-permute-start.1 = (f32[512,768]{1,0:T(8,128)S(1)}, f32[512,768]{1,0:T(8,128)S(1)}, u32[]{:S(2)}, u32[]{:S(2)}) collective-permute-start(f32[512,768]{1,0:T(8,128)S(1)} %multiply_reduce_fusion.2), channel_id=1, source_target_pairs={{0,1},{1,0},{2,3},{3,2},{4,5},{5,4},{6,7},{7,6},{8,9},{9,8},{10,11... | collective-permute-start | bytes 4718600 | tf_op jit(solution)/shard_map/ppermute | solution.py:44
  224.9 2.2 copy-start.1
  233.6 8.0 %collective-permute-start.2 = (f32[512,768]{1,0:T(8,128)S(1)}, f32[512,768]{1,0:T(8,128)S(1)}, u32[]{:S(2)}, u32[]{:S(2)}) collective-permute-start(f32[512,768]{1,0:T(8,128)S(1)} %multiply_reduce_fusion), channel_id=1, source_target_pairs={{0,1},{1,0},{2,3},{3,2},{4,5},{5,4},{6,7},{7,6},{8,9},{9,8},{10,11... | collective-permute-start | bytes 4718600 | tf_op jit(solution)/shard_map/ppermute | solution.py:44
  233.7 35.6 %collective-permute-start.3 = (f32[512,768]{1,0:T(8,128)S(1)}, f32[512,768]{1,0:T(8,128)S(1)}, u32[]{:S(2)}, u32[]{:S(2)}) collective-permute-start(f32[512,768]{1,0:T(8,128)S(1)} %add.63), channel_id=1, source_target_pairs={{0,2},{2,0},{1,3},{3,1},{4,6},{6,4},{5,7},{7,5},{8,10},{10,8},{9,1... | collective-permute-start | bytes 4718600 | tf_op jit(solution)/shard_map/ppermute | solution.py:49
Sparse Core Ops, SparseCore 0:
  20.3 187.4 all-gather.1

commit v7 on v6

--- a/solution.py
+++ b/solution.py
@@ -33,22 +33,28 @@
     quarter = w_full.shape[2] // 2
     xl, c = lax.axis_index("xl"), lax.axis_index("c")
 
-    def terms(rows, scale, h, part):
-        w_part = lax.dynamic_slice_in_dim(w_full[(h + xh) % 2], part * quarter, quarter, axis=1)
+    def terms(rows, scale, h, part, lo=0, size=quarter):
+        w_part = lax.dynamic_slice_in_dim(w_full[(h + xh) % 2], part * quarter + lo, size, axis=1)
         out = lax.dot_general(
             rows, w_part, (((2,), (2,)), ((0,), (0,))), preferred_element_type=jnp.float32
         )
         return jnp.sum(scale[:, :, None] * out, axis=0)
 
-    def by_core(rows, scale, h):
-        sent = lax.ppermute(terms(rows, scale, h, 1 - c), "c", perm=SWAP)
-        return terms(rows, scale, h, c) + sent
+    def by_core(rows, scale, h, lo=0, size=quarter):
+        sent = lax.ppermute(terms(rows, scale, h, 1 - c, lo, size), "c", perm=SWAP)
+        return terms(rows, scale, h, c, lo, size) + sent
 
-    far = by_core(rows, scale, 1 - xl)
-    near_rows, near_scale, far = lax.optimization_barrier((rows, scale, far))
-    far = lax.ppermute(far, "xl", perm=SWAP)
+    widths = (quarter // 6, quarter // 3)
+    widths = widths + (quarter - sum(widths),)
+    sent_far, lo = [], 0
+    for width in widths:
+        piece = by_core(rows, scale, 1 - xl, lo, width)
+        sent_far.append(lax.ppermute(piece, "xl", perm=SWAP))
+        rows, scale, piece = lax.optimization_barrier((rows, scale, piece))
+        lo += width
+    near_rows, near_scale = rows, scale
     near = by_core(near_rows, near_scale, xl)
-    mixed = near + far
+    mixed = near + jnp.concatenate(sent_far, axis=1)
     return mixed.astype(jnp.bfloat16)
 
 

time: 278 us -> 287 us (1.032)
  matrix products: 36.6 us -> 47.5 us
  waiting for transfers between devices: 213 us -> 210 us
    dot_general x4 -> x8, matrix products: 28.4 us -> 39.3 us  [terms(): lax.dot_general(rows, w_part, (((2,), (2,)), ((0,), (0,))), preferred_ele...]
    ppermute x3 -> x7, waiting for transfers between devices: 27.7 us -> 25.1 us  [the longest x3 25.1 us: body(): sent_far.append(lax.ppermute(piece, 'xl', perm=SWAP))]
  transfers between devices with their start and end apart: 5 -> 9, of which waited for: 3 -> 4; matrix products, arithmetic and copies ran while one was open for 9% -> 11% of each run, Pallas kernels for 0% -> 0%
where the time goes in v7:
time: 287 us; the launch traced here: 286 us
  waiting for transfers between devices  210 us (73%)
  matrix products  47.5 us (17%)
  between operations  13.5 us (5%)
  starting transfers between devices  8.6 us (3%)
  other arithmetic  6.67 us (2%)
    all_gather x1, waiting for transfers between devices, body(): w_full = lax.all_gather(pair, ('z', 'y'), axis=2, tiled=True)  177 us
    dot_general x8, matrix products, terms(): lax.dot_general(rows, w_part, (((2,), (2,)), ((0,), (0,))), preferred_ele...  39.3 us
    ppermute x3, waiting for transfers between devices, body(): sent_far.append(lax.ppermute(piece, 'xl', perm=SWAP))  25.1 us
    dot_general x1, matrix products, body(): lax.dot_general(pick.astype(hidden.dtype), hidden, (((2,), (0,)), ((), ()...  8.19 us
    ppermute x1, waiting for transfers between devices, body(): partner = lax.ppermute(down_weight, 'xh', perm=SWAP)  8.11 us
  transfers between devices with their start and end apart: 9, of which 4 were waited for; matrix products, arithmetic and copies ran while one was open for 11% of the time, Pallas kernels for 0%

profile of v7, /device:TPU:1, one launch (start us, length us, event | category | flops | bytes accessed | tf_op | source)
XLA Modules:
  0.0 286.4 jit_solution(17347583406504302252)
XLA Ops:
  6.5 0.0 copy-start
  6.5 0.0 all-gather.2.cloned.1.call-start
  6.5 3.6 %collective-permute-start = (bf16[2,48,2048]{2,1,0:T(8,128)(2,1)}, bf16[2,48,2048]{2,1,0:T(8,128)(2,1)S(1)}, u32[]{:S(2)}, u32[]{:S(2)}) collective-permute-start(bf16[2,48,2048]{2,1,0:T(8,128)(2,1)} %param.6), channel_id=1, source_target_pairs={{0,128},{128,0},{1,129},{129,1},{2,130},{130,2},{3,131},{131,3},{4... | collective-permute-start | bytes 1179656 | tf_op jit(solution)/shard_map/ppermute | solution.py:17
  10.1 8.1 %collective-permute-done = bf16[2,48,2048]{2,1,0:T(8,128)(2,1)S(1)} collective-permute-done((bf16[2,48,2048]{2,1,0:T(8,128)(2,1)}, bf16[2,48,2048]{2,1,0:T(8,128)(2,1)S(1)}, u32[]{:S(2)}, u32[]{:S(2)}) %collective-permute-start) | collective-permute-done | bytes 393248 | tf_op jit(solution)/shard_map/ppermute | solution.py:17
  18.2 1.9 pad_maximum_fusion
  20.2 0.0 all-gather.2.cloned.1.call-update
  20.2 0.0 copy-done
  20.2 0.1 broadcast_bitcast_fusion
  20.3 1.0 iota_compare_fusion
  21.3 1.5 fusion.8
  22.8 8.2 %fusion.10 = bf16[2,512,2048]{2,1,0:T(8,128)(2,1)} fusion(bf16[1024,2048]{1,0:T(8,128)(2,1)} %param.5, pred[2,1024]{1,0:T(4,128)(4,1)S(1)} %iota_compare_fusion.1, pred[512,1024]{1,0:T(8,128)(4,1)S(1)} %iota_compare_fusion), kind=kOutput, calls=%fused_computation.11 | convolution fusion | flops 4298113024 | bytes 8914944 | tf_op jit(solution)/shard_map/dot_general | solution.py:28
  31.0 176.8 %all-gather.2.cloned.1.call-done = bf16[2,2,1536,2048]{3,2,1,0:T(8,128)(2,1)} async-done(((bf16[2,2,48,2048]{3,2,1,0:T(8,128)(2,1)}), bf16[2,2,1536,2048]{3,2,1,0:T(8,128)(2,1)}) %all-gather.2.cloned.1.call-update) | async-done | bytes 25165840 | tf_op jit(solution)/shard_map/all_gather | solution.py:19
  207.8 0.0 copy-start.1
  207.8 3.9 %fusion.51 = f32[512,128]{1,0:T(8,128)S(1)} fusion(bf16[2,512,2048]{2,1,0:T(8,128)(2,1)} %fusion.10, bf16[2,2,1536,2048]{3,2,1,0:T(8,128)(2,1)} %all-gather.2.cloned.1.call-done, s32[]{:T(128)S(6)} %select_n.82, s32[]{:T(128)S(6)} %select_n.86, f32[2,512]{1,0:T(2,128)S(1)} %fusion.8), kind=kOutput, calls=%fused_computation.40 | convolution fusion | flops 537067520 | bytes 5509128 | tf_op jit(solution)/shard_map/dot_general | solution.py:38
  211.8 1.5 collective-permute-start.1
  213.2 0.0 copy-done.1
  213.2 2.5 fusion.50
  215.8 0.0 collective-permute-done.1
  215.8 3.0 %fusion.44 = f32[512,256]{1,0:T(8,128)S(1)} fusion(bf16[2,512,2048]{2,1,0:T(8,128)(2,1)S(1)} %copy-done.1, bf16[2,2,1536,2048]{3,2,1,0:T(8,128)(2,1)} %all-gather.2.cloned.1.call-done, s32[]{:T(128)S(6)} %select_n.82, s32[]{:T(128)S(6)} %select_n.90, f32[2,512]{1,0:T(2,128)S(1)} %fusion.8), kind=kOutput, calls=%fused_computation.35 | convolution fusion | flops 1074135040 | bytes 6819848 | tf_op jit(solution)/shard_map/dot_general | solution.py:38
  218.8 0.3 collective-permute-start.2
  219.1 0.0 copy-start.2
  219.1 4.4 %fusion.47 = f32[512,256]{1,0:T(8,128)S(1)} fusion(bf16[2,512,2048]{2,1,0:T(8,128)(2,1)} %fusion.10, bf16[2,2,1536,2048]{3,2,1,0:T(8,128)(2,1)} %all-gather.2.cloned.1.call-done, s32[]{:T(128)S(6)} %select_n.82, s32[]{:T(128)S(6)} %select_n.88, f32[2,512]{1,0:T(2,128)S(1)} %fusion.8), kind=kOutput, calls=%fused_computation.36 | convolution fusion | flops 1074135040 | bytes 6819848 | tf_op jit(solution)/shard_map/dot_general | solution.py:38
  223.5 0.0 collective-permute-done.2
  223.5 0.9 add.134
  224.3 0.0 copy-done.2
  224.4 4.4 %multiply_reduce_fusion.2 = f32[512,384]{1,0:T(8,128)S(1)} fusion(bf16[2,512,2048]{2,1,0:T(8,128)(2,1)S(1)} %copy-done.2, bf16[2,2,1536,2048]{3,2,1,0:T(8,128)(2,1)} %all-gather.2.cloned.1.call-done, s32[]{:T(128)S(6)} %select_n.82, s32[]{:T(128)S(6)} %select_n.94, f32[2,512]{1,0:T(2,128)S(1)} %fusion.8), kind=kOutput, calls=%fused_computation.31 | convolution fusion | flops 1611202560 | bytes 8130568 | tf_op jit(solution)/shard_map/dot_general | solution.py:38
  228.7 0.5 collective-permute-start.3
  229.3 0.0 copy-start.3
  229.3 5.7 %multiply_reduce_fusion.3 = f32[512,384]{1,0:T(8,128)S(1)} fusion(bf16[2,512,2048]{2,1,0:T(8,128)(2,1)} %fusion.10, bf16[2,2,1536,2048]{3,2,1,0:T(8,128)(2,1)} %all-gather.2.cloned.1.call-done, s32[]{:T(128)S(6)} %select_n.82, s32[]{:T(128)S(6)} %select_n.92, f32[2,512]{1,0:T(2,128)S(1)} %fusion.8), kind=kOutput, calls=%fused_computation.32 | convolution fusion | flops 1611202560 | bytes 8130568 | tf_op jit(solution)/shard_map/dot_general | solution.py:38
  235.0 0.0 collective-permute-done.3
  235.0 0.1 add.139
  235.1 0.0 copy-done.3
  235.1 7.6 %multiply_reduce_fusion = f32[512,768]{1,0:T(8,128)} fusion(f32[2,512]{1,0:T(2,128)S(1)} %fusion.8, bf16[2,512,2048]{2,1,0:T(8,128)(2,1)S(1)} %copy-done.3, bf16[2,2,1536,2048]{3,2,1,0:T(8,128)(2,1)} %all-gather.2.cloned.1.call-done, s32[]{:T(128)S(6)} %select_n.97, s32[]{:T(128)S(6)} %select_n.99), kind=kOutput, calls=%fused_computation.16 | convolution fusion | flops 3222405120 | bytes 12062728 | tf_op jit(solution)/shard_map/dot_general | solution.py:38
  242.8 0.1 collective-permute-start.4
  242.8 1.2 collective-permute-start.7
  244.0 0.3 collective-permute-start.5
  244.3 1.2 collective-permute-start.6
  245.5 7.8 %multiply_reduce_fusion.1 = f32[512,768]{1,0:T(8,128)S(1)} fusion(f32[2,512]{1,0:T(2,128)S(1)} %fusion.8, bf16[2,512,2048]{2,1,0:T(8,128)(2,1)} %fusion.10, bf16[2,2,1536,2048]{3,2,1,0:T(8,128)(2,1)} %all-gather.2.cloned.1.call-done, s32[]{:T(128)S(6)} %select_n.97, s32[]{:T(128)S(6)} %select_n.98), kind=kOutput, calls=%fused_computation.17 | convolution fusion | flops 3222405120 | bytes 12062728 | tf_op jit(solution)/shard_map/dot_general | solution.py:38
  253.3 13.9 %collective-permute-done.5 = f32[512,128]{1,0:T(8,128)S(1)} collective-permute-done((f32[512,128]{1,0:T(8,128)S(1)}, f32[512,128]{1,0:T(8,128)S(1)}, u32[]{:S(2)}, u32[]{:S(2)}) %collective-permute-start.5) | collective-permute-done | bytes 262176 | tf_op jit(solution)/shard_map/ppermute | solution.py:52
  267.1 11.2 %collective-permute-done.6 = f32[512,256]{1,0:T(8,128)S(1)} collective-permute-done((f32[512,256]{1,0:T(8,128)}, f32[512,256]{1,0:T(8,128)S(1)}, u32[]{:S(2)}, u32[]{:S(2)}) %collective-permute-start.6) | collective-permute-done | bytes 524320 | tf_op jit(solution)/shard_map/ppermute | solution.py:52
  278.3 0.0 collective-permute-done.7
  278.3 0.0 collective-permute-done.4
  278.4 1.2 fusion.29
  (2 shorter events, 0.0 us)
Async XLA Ops:
  6.5 13.7 %copy-start = (s32[8]{0:T(128)S(1)}, s32[8]{0:T(128)}, u32[]{:S(2)}) copy-start(s32[8]{0:T(128)} %param.7) | copy-start | bytes 100
  6.5 201.3 %all-gather.2.cloned.1.call-start = ((), (), s32[]{:S(2)}) async-start(), calls=%async_computation | async-start | bytes 25952256 | tf_op jit(solution)/shard_map/all_gather | solution.py:19
  6.5 11.7 %collective-permute-start = (bf16[2,48,2048]{2,1,0:T(8,128)(2,1)}, bf16[2,48,2048]{2,1,0:T(8,128)(2,1)S(1)}, u32[]{:S(2)}, u32[]{:S(2)}) collective-permute-start(bf16[2,48,2048]{2,1,0:T(8,128)(2,1)} %param.6), channel_id=1, source_target_pairs={{0,128},{128,0},{1,129},{129,1},{2,130},{130,2},{3,131},{131,3},{4... | collective-permute-start | bytes 1179656 | tf_op jit(solution)/shard_map/ppermute | solution.py:17
  207.8 5.4 %copy-start.1 = (bf16[2,512,2048]{2,1,0:T(8,128)(2,1)S(1)}, bf16[2,512,2048]{2,1,0:T(8,128)(2,1)}, u32[]{:S(2)}) copy-start(bf16[2,512,2048]{2,1,0:T(8,128)(2,1)} %fusion.10) | copy-start | bytes 12582916
  211.8 4.0 %collective-permute-start.1 = (f32[512,128]{1,0:T(8,128)S(1)}, f32[512,128]{1,0:T(8,128)S(1)}, u32[]{:S(2)}, u32[]{:S(2)}) collective-permute-start(f32[512,128]{1,0:T(8,128)S(1)} %fusion.51), channel_id=1, source_target_pairs={{0,1},{1,0},{2,3},{3,2},{4,5},{5,4},{6,7},{7,6},{8,9},{9,8},{10,11... | collective-permute-start | bytes 786440 | tf_op jit(solution)/shard_map/ppermute | solution.py:44
  218.8 4.7 %collective-permute-start.2 = (f32[512,256]{1,0:T(8,128)S(1)}, f32[512,256]{1,0:T(8,128)S(1)}, u32[]{:S(2)}, u32[]{:S(2)}) collective-permute-start(f32[512,256]{1,0:T(8,128)S(1)} %fusion.44), channel_id=1, source_target_pairs={{0,1},{1,0},{2,3},{3,2},{4,5},{5,4},{6,7},{7,6},{8,9},{9,8},{10,11... | collective-permute-start | bytes 1572872 | tf_op jit(solution)/shard_map/ppermute | solution.py:44
  219.1 5.3 %copy-start.2 = (bf16[2,512,2048]{2,1,0:T(8,128)(2,1)S(1)}, bf16[2,512,2048]{2,1,0:T(8,128)(2,1)}, u32[]{:S(2)}) copy-start(bf16[2,512,2048]{2,1,0:T(8,128)(2,1)} %fusion.10) | copy-start | bytes 12582916
  228.7 6.3 %collective-permute-start.3 = (f32[512,384]{1,0:T(8,128)S(1)}, f32[512,384]{1,0:T(8,128)S(1)}, u32[]{:S(2)}, u32[]{:S(2)}) collective-permute-start(f32[512,384]{1,0:T(8,128)S(1)} %multiply_reduce_fusion.2), channel_id=1, source_target_pairs={{0,1},{1,0},{2,3},{3,2},{4,5},{5,4},{6,7},{7,6},{8,9},{9,8},{10,11... | collective-permute-start | bytes 2359304 | tf_op jit(solution)/shard_map/ppermute | solution.py:44
  229.3 5.9 %copy-start.3 = (bf16[2,512,2048]{2,1,0:T(8,128)(2,1)S(1)}, bf16[2,512,2048]{2,1,0:T(8,128)(2,1)}, u32[]{:S(2)}) copy-start(bf16[2,512,2048]{2,1,0:T(8,128)(2,1)} %fusion.10) | copy-start | bytes 12582916
  242.8 35.6 %collective-permute-start.4 = (f32[512,768]{1,0:T(8,128)}, f32[512,768]{1,0:T(8,128)S(1)}, u32[]{:S(2)}, u32[]{:S(2)}) collective-permute-start(f32[512,768]{1,0:T(8,128)} %multiply_reduce_fusion), channel_id=1, source_target_pairs={{0,1},{1,0},{2,3},{3,2},{4,5},{5,4},{6,7},{7,6},{8,9},{9,8},{10,11... | collective-permute-start | bytes 4718600 | tf_op jit(solution)/shard_map/ppermute | solution.py:44
  242.8 35.5 %collective-permute-start.7 = (f32[512,384]{1,0:T(8,128)S(1)}, f32[512,384]{1,0:T(8,128)S(1)}, u32[]{:S(2)}, u32[]{:S(2)}) collective-permute-start(f32[512,384]{1,0:T(8,128)S(1)} %add.139), channel_id=1, source_target_pairs={{0,2},{2,0},{1,3},{3,1},{4,6},{6,4},{5,7},{7,5},{8,10},{10,8},{9,1... | collective-permute-start | bytes 2359304 | tf_op jit(solution)/shard_map/ppermute | solution.py:52
  244.0 23.1 %collective-permute-start.5 = (f32[512,128]{1,0:T(8,128)S(1)}, f32[512,128]{1,0:T(8,128)S(1)}, u32[]{:S(2)}, u32[]{:S(2)}) collective-permute-start(f32[512,128]{1,0:T(8,128)S(1)} %add.129), channel_id=1, source_target_pairs={{0,2},{2,0},{1,3},{3,1},{4,6},{6,4},{5,7},{7,5},{8,10},{10,8},{9,1... | collective-permute-start | bytes 786440 | tf_op jit(solution)/shard_map/ppermute | solution.py:52
  244.3 34.0 %collective-permute-start.6 = (f32[512,256]{1,0:T(8,128)}, f32[512,256]{1,0:T(8,128)S(1)}, u32[]{:S(2)}, u32[]{:S(2)}) collective-permute-start(f32[512,256]{1,0:T(8,128)} %add.134), channel_id=1, source_target_pairs={{0,2},{2,0},{1,3},{3,1},{4,6},{6,4},{5,7},{7,5},{8,10},{10,8},{9,1... | collective-permute-start | bytes 1572872 | tf_op jit(solution)/shard_map/ppermute | solution.py:52
Sparse Core Ops, SparseCore 0:
  20.3 187.4 all-gather.1

commit v8 on v7

--- a/solution.py
+++ b/solution.py
@@ -44,18 +44,19 @@
         sent = lax.ppermute(terms(rows, scale, h, 1 - c, lo, size), "c", perm=SWAP)
         return terms(rows, scale, h, c, lo, size) + sent
 
-    widths = (quarter // 6, quarter // 3)
-    widths = widths + (quarter - sum(widths),)
-    sent_far, lo = [], 0
-    for width in widths:
-        piece = by_core(rows, scale, 1 - xl, lo, width)
-        sent_far.append(lax.ppermute(piece, "xl", perm=SWAP))
-        rows, scale, piece = lax.optimization_barrier((rows, scale, piece))
-        lo += width
-    near_rows, near_scale = rows, scale
+    piece = quarter // 3
+    first = by_core(rows, scale, 1 - xl, 0, piece)
+    first_far = lax.ppermute(first, "xl", perm=SWAP)
+    rows, scale, first = lax.optimization_barrier((rows, scale, first))
+    second = by_core(rows, scale, 1 - xl, piece, quarter - piece)
+    near_rows, near_scale, second = lax.optimization_barrier((rows, scale, second))
+    second_far = lax.ppermute(second, "xl", perm=SWAP)
     near = by_core(near_rows, near_scale, xl)
-    mixed = near + jnp.concatenate(sent_far, axis=1)
-    return mixed.astype(jnp.bfloat16)
+    mixed = [
+        (near[:, :piece] + first_far).astype(jnp.bfloat16),
+        (near[:, piece:] + second_far).astype(jnp.bfloat16),
+    ]
+    return jnp.concatenate(mixed, axis=1)
 
 
 def solution(mesh):

time: 287 us -> 282 us (0.983)
  matrix products: 47.5 us -> 43.1 us
    dot_general x8 -> x6, matrix products: 39.3 us -> 34.9 us  [terms(): lax.dot_general(rows, w_part, (((2,), (2,)), ((0,), (0,))), preferred_ele...]
    ppermute x3 -> x2, waiting for transfers between devices: 25.1 us -> 25.1 us  [the longest x1 15.3 us: body(): second_far = lax.ppermute(second, 'xl', perm=SWAP)]
  transfers between devices with their start and end apart: 9 -> 7, of which waited for: 4 -> 4; matrix products, arithmetic and copies ran while one was open for 11% -> 11% of each run, Pallas kernels for 0% -> 0%
where the time goes in v8:
time: 282 us; the launch traced here: 281 us
  waiting for transfers between devices  210 us (74%)
  matrix products  43.1 us (15%)
  between operations  13.6 us (5%)
  other arithmetic  7.33 us (3%)
  starting transfers between devices  7.26 us (3%)
    all_gather x1, waiting for transfers between devices, body(): w_full = lax.all_gather(pair, ('z', 'y'), axis=2, tiled=True)  177 us
    dot_general x6, matrix products, terms(): lax.dot_general(rows, w_part, (((2,), (2,)), ((0,), (0,))), preferred_ele...  34.9 us
    ppermute x1, waiting for transfers between devices, body(): second_far = lax.ppermute(second, 'xl', perm=SWAP)  15.3 us
    ppermute x1, waiting for transfers between devices, body(): first_far = lax.ppermute(first, 'xl', perm=SWAP)  9.76 us
    dot_general x1, matrix products, body(): lax.dot_general(pick.astype(hidden.dtype), hidden, (((2,), (0,)), ((), ()...  8.19 us
    ppermute x1, waiting for transfers between devices, body(): partner = lax.ppermute(down_weight, 'xh', perm=SWAP)  8.11 us
  transfers between devices with their start and end apart: 7, of which 4 were waited for; matrix products, arithmetic and copies ran while one was open for 11% of the time, Pallas kernels for 0%

profile of v8, /device:TPU:1, one launch (start us, length us, event | category | flops | bytes accessed | tf_op | source)
XLA Modules:
  0.0 281.4 jit_solution(12821226490104743296)
XLA Ops:
  6.5 0.0 copy-start
  6.5 0.0 all-gather.2.cloned.1.call-start
  6.5 3.6 %collective-permute-start = (bf16[2,48,2048]{2,1,0:T(8,128)(2,1)}, bf16[2,48,2048]{2,1,0:T(8,128)(2,1)S(1)}, u32[]{:S(2)}, u32[]{:S(2)}) collective-permute-start(bf16[2,48,2048]{2,1,0:T(8,128)(2,1)} %param.6), channel_id=1, source_target_pairs={{0,128},{128,0},{1,129},{129,1},{2,130},{130,2},{3,131},{131,3},{4... | collective-permute-start | bytes 1179656 | tf_op jit(solution)/shard_map/ppermute | solution.py:17
  10.1 8.1 %collective-permute-done = bf16[2,48,2048]{2,1,0:T(8,128)(2,1)S(1)} collective-permute-done((bf16[2,48,2048]{2,1,0:T(8,128)(2,1)}, bf16[2,48,2048]{2,1,0:T(8,128)(2,1)S(1)}, u32[]{:S(2)}, u32[]{:S(2)}) %collective-permute-start) | collective-permute-done | bytes 393248 | tf_op jit(solution)/shard_map/ppermute | solution.py:17
  18.2 1.9 pad_maximum_fusion
  20.2 0.0 all-gather.2.cloned.1.call-update
  20.2 0.0 copy-done
  20.2 0.1 broadcast_bitcast_fusion
  20.3 1.0 iota_compare_fusion
  21.3 1.5 fusion.8
  22.8 8.2 %fusion.16 = bf16[2,512,2048]{2,1,0:T(8,128)(2,1)} fusion(bf16[1024,2048]{1,0:T(8,128)(2,1)} %param.5, pred[2,1024]{1,0:T(4,128)(4,1)S(1)} %iota_compare_fusion.1, pred[512,1024]{1,0:T(8,128)(4,1)S(1)} %iota_compare_fusion), kind=kOutput, calls=%fused_computation.17 | convolution fusion | flops 4298113024 | bytes 8914944 | tf_op jit(solution)/shard_map/dot_general | solution.py:28
  31.0 176.8 %all-gather.2.cloned.1.call-done = bf16[2,2,1536,2048]{3,2,1,0:T(8,128)(2,1)} async-done(((bf16[2,2,48,2048]{3,2,1,0:T(8,128)(2,1)}), bf16[2,2,1536,2048]{3,2,1,0:T(8,128)(2,1)}) %all-gather.2.cloned.1.call-update) | async-done | bytes 25165840 | tf_op jit(solution)/shard_map/all_gather | solution.py:19
  207.8 4.2 %fusion.43 = f32[512,256]{1,0:T(8,128)S(1)} fusion(bf16[2,512,2048]{2,1,0:T(8,128)(2,1)} %fusion.16, bf16[2,2,1536,2048]{3,2,1,0:T(8,128)(2,1)} %all-gather.2.cloned.1.call-done, s32[]{:T(128)S(6)} %select_n.66, s32[]{:T(128)S(6)} %select_n.70, f32[2,512]{1,0:T(2,128)S(1)} %fusion.8), kind=kOutput, calls=%fused_computation.33 | convolution fusion | flops 1074135040 | bytes 6819848 | tf_op jit(solution)/shard_map/dot_general | solution.py:38
  212.0 1.5 collective-permute-start.1
  213.5 0.0 copy-start.1
  213.5 4.4 %fusion.46 = f32[512,256]{1,0:T(8,128)S(1)} fusion(bf16[2,512,2048]{2,1,0:T(8,128)(2,1)} %fusion.16, bf16[2,2,1536,2048]{3,2,1,0:T(8,128)(2,1)} %all-gather.2.cloned.1.call-done, s32[]{:T(128)S(6)} %select_n.66, s32[]{:T(128)S(6)} %select_n.68, f32[2,512]{1,0:T(2,128)S(1)} %fusion.8), kind=kOutput, calls=%fused_computation.34 | convolution fusion | flops 1074135040 | bytes 6819848 | tf_op jit(solution)/shard_map/dot_general | solution.py:38
  217.9 0.0 collective-permute-done.1
  217.9 0.1 add.99
  218.0 0.0 copy-done.1
  218.0 4.9 %multiply_reduce_fusion.2 = f32[512,512]{1,0:T(8,128)S(1)} fusion(bf16[2,512,2048]{2,1,0:T(8,128)(2,1)S(1)} %copy-done.1, bf16[2,2,1536,2048]{3,2,1,0:T(8,128)(2,1)} %all-gather.2.cloned.1.call-done, s32[]{:T(128)S(6)} %select_n.66, s32[]{:T(128)S(6)} %select_n.74, f32[2,512]{1,0:T(2,128)S(1)} %fusion.8), kind=kOutput, calls=%fused_computation.24 | convolution fusion | flops 2148270080 | bytes 9441288 | tf_op jit(solution)/shard_map/dot_general | solution.py:38
  222.9 0.3 collective-permute-start.2
  223.2 0.0 copy-start.2
  223.2 6.1 %multiply_reduce_fusion.3 = f32[512,512]{1,0:T(8,128)S(1)} fusion(bf16[2,512,2048]{2,1,0:T(8,128)(2,1)} %fusion.16, bf16[2,2,1536,2048]{3,2,1,0:T(8,128)(2,1)} %all-gather.2.cloned.1.call-done, s32[]{:T(128)S(6)} %select_n.66, s32[]{:T(128)S(6)} %select_n.72, f32[2,512]{1,0:T(2,128)S(1)} %fusion.8), kind=kOutput, calls=%fused_computation.25 | convolution fusion | flops 2148270080 | bytes 9441288 | tf_op jit(solution)/shard_map/dot_general | solution.py:38
  229.3 0.0 collective-permute-done.2
  229.3 0.2 add.104
  229.5 0.0 copy-done.2
  229.5 7.6 %multiply_reduce_fusion = f32[512,768]{1,0:T(8,128)} fusion(f32[2,512]{1,0:T(2,128)S(1)} %fusion.8, bf16[2,512,2048]{2,1,0:T(8,128)(2,1)S(1)} %copy-done.2, bf16[2,2,1536,2048]{3,2,1,0:T(8,128)(2,1)} %all-gather.2.cloned.1.call-done, s32[]{:T(128)S(6)} %select_n.77, s32[]{:T(128)S(6)} %select_n.79), kind=kOutput, calls=%fused_computation.18 | convolution fusion | flops 3222405120 | bytes 12062728 | tf_op jit(solution)/shard_map/dot_general | solution.py:38
  237.1 0.5 collective-permute-start.3
  237.6 1.2 collective-permute-start.5
  238.8 0.3 collective-permute-start.4
  239.1 7.8 %multiply_reduce_fusion.1 = f32[512,768]{1,0:T(8,128)S(1)} fusion(f32[2,512]{1,0:T(2,128)S(1)} %fusion.8, bf16[2,512,2048]{2,1,0:T(8,128)(2,1)} %fusion.16, bf16[2,2,1536,2048]{3,2,1,0:T(8,128)(2,1)} %all-gather.2.cloned.1.call-done, s32[]{:T(128)S(6)} %select_n.77, s32[]{:T(128)S(6)} %select_n.78), kind=kOutput, calls=%fused_computation.19 | convolution fusion | flops 3222405120 | bytes 12062728 | tf_op jit(solution)/shard_map/dot_general | solution.py:38
  246.8 0.0 collective-permute-done.3
  246.9 0.2 add.108
  247.1 15.3 %collective-permute-done.5 = f32[512,512]{1,0:T(8,128)} collective-permute-done((f32[512,512]{1,0:T(8,128)S(1)}, f32[512,512]{1,0:T(8,128)}, u32[]{:S(2)}, u32[]{:S(2)}) %collective-permute-start.5) | collective-permute-done | bytes 1048608 | tf_op jit(solution)/shard_map/ppermute | solution.py:53
  262.4 1.4 fusion.49
  263.7 9.8 %collective-permute-done.4 = f32[512,256]{1,0:T(8,128)S(1)} collective-permute-done((f32[512,256]{1,0:T(8,128)S(1)}, f32[512,256]{1,0:T(8,128)S(1)}, u32[]{:S(2)}, u32[]{:S(2)}) %collective-permute-start.4) | collective-permute-done | bytes 524320 | tf_op jit(solution)/shard_map/ppermute | solution.py:49
  273.5 0.1 fusion.50
  273.6 0.9 pad_maximum_fusion.1
  (1 shorter events, 0.0 us)
Async XLA Ops:
  6.5 13.7 %copy-start = (s32[8]{0:T(128)S(1)}, s32[8]{0:T(128)}, u32[]{:S(2)}) copy-start(s32[8]{0:T(128)} %param.7) | copy-start | bytes 100
  6.5 201.3 %all-gather.2.cloned.1.call-start = ((), (), s32[]{:S(2)}) async-start(), calls=%async_computation | async-start | bytes 25952256 | tf_op jit(solution)/shard_map/all_gather | solution.py:19
  6.5 11.7 %collective-permute-start = (bf16[2,48,2048]{2,1,0:T(8,128)(2,1)}, bf16[2,48,2048]{2,1,0:T(8,128)(2,1)S(1)}, u32[]{:S(2)}, u32[]{:S(2)}) collective-permute-start(bf16[2,48,2048]{2,1,0:T(8,128)(2,1)} %param.6), channel_id=1, source_target_pairs={{0,128},{128,0},{1,129},{129,1},{2,130},{130,2},{3,131},{131,3},{4... | collective-permute-start | bytes 1179656 | tf_op jit(solution)/shard_map/ppermute | solution.py:17
  212.0 5.9 %collective-permute-start.1 = (f32[512,256]{1,0:T(8,128)S(1)}, f32[512,256]{1,0:T(8,128)S(1)}, u32[]{:S(2)}, u32[]{:S(2)}) collective-permute-start(f32[512,256]{1,0:T(8,128)S(1)} %fusion.43), channel_id=1, source_target_pairs={{0,1},{1,0},{2,3},{3,2},{4,5},{5,4},{6,7},{7,6},{8,9},{9,8},{10,11... | collective-permute-start | bytes 1572872 | tf_op jit(solution)/shard_map/ppermute | solution.py:44
  213.5 4.5 %copy-start.1 = (bf16[2,512,2048]{2,1,0:T(8,128)(2,1)S(1)}, bf16[2,512,2048]{2,1,0:T(8,128)(2,1)}, u32[]{:S(2)}) copy-start(bf16[2,512,2048]{2,1,0:T(8,128)(2,1)} %fusion.16) | copy-start | bytes 12582916
  222.9 6.4 %collective-permute-start.2 = (f32[512,512]{1,0:T(8,128)S(1)}, f32[512,512]{1,0:T(8,128)S(1)}, u32[]{:S(2)}, u32[]{:S(2)}) collective-permute-start(f32[512,512]{1,0:T(8,128)S(1)} %multiply_reduce_fusion.2), channel_id=1, source_target_pairs={{0,1},{1,0},{2,3},{3,2},{4,5},{5,4},{6,7},{7,6},{8,9},{9,8},{10,11... | collective-permute-start | bytes 3145736 | tf_op jit(solution)/shard_map/ppermute | solution.py:44
  223.2 6.3 %copy-start.2 = (bf16[2,512,2048]{2,1,0:T(8,128)(2,1)S(1)}, bf16[2,512,2048]{2,1,0:T(8,128)(2,1)}, u32[]{:S(2)}) copy-start(bf16[2,512,2048]{2,1,0:T(8,128)(2,1)} %fusion.16) | copy-start | bytes 12582916
  237.1 9.7 %collective-permute-start.3 = (f32[512,768]{1,0:T(8,128)}, f32[512,768]{1,0:T(8,128)S(1)}, u32[]{:S(2)}, u32[]{:S(2)}) collective-permute-start(f32[512,768]{1,0:T(8,128)} %multiply_reduce_fusion), channel_id=1, source_target_pairs={{0,1},{1,0},{2,3},{3,2},{4,5},{5,4},{6,7},{7,6},{8,9},{9,8},{10,11... | collective-permute-start | bytes 4718600 | tf_op jit(solution)/shard_map/ppermute | solution.py:44
  237.6 24.8 %collective-permute-start.5 = (f32[512,512]{1,0:T(8,128)S(1)}, f32[512,512]{1,0:T(8,128)}, u32[]{:S(2)}, u32[]{:S(2)}) collective-permute-start(f32[512,512]{1,0:T(8,128)S(1)} %add.104), channel_id=1, source_target_pairs={{0,2},{2,0},{1,3},{3,1},{4,6},{6,4},{5,7},{7,5},{8,10},{10,8},{9,1... | collective-permute-start | bytes 3145736 | tf_op jit(solution)/shard_map/ppermute | solution.py:53
  238.8 34.7 %collective-permute-start.4 = (f32[512,256]{1,0:T(8,128)S(1)}, f32[512,256]{1,0:T(8,128)S(1)}, u32[]{:S(2)}, u32[]{:S(2)}) collective-permute-start(f32[512,256]{1,0:T(8,128)S(1)} %add.99), channel_id=1, source_target_pairs={{0,2},{2,0},{1,3},{3,1},{4,6},{6,4},{5,7},{7,5},{8,10},{10,8},{9,1... | collective-permute-start | bytes 1572872 | tf_op jit(solution)/shard_map/ppermute | solution.py:49
Sparse Core Ops, SparseCore 0:
  20.3 187.4 all-gather.1

commit v9 on v8

--- a/solution.py
+++ b/solution.py
@@ -44,7 +44,7 @@
         sent = lax.ppermute(terms(rows, scale, h, 1 - c, lo, size), "c", perm=SWAP)
         return terms(rows, scale, h, c, lo, size) + sent
 
-    piece = quarter // 3
+    piece = quarter // 6
     first = by_core(rows, scale, 1 - xl, 0, piece)
     first_far = lax.ppermute(first, "xl", perm=SWAP)
     rows, scale, first = lax.optimization_barrier((rows, scale, first))
@@ -52,11 +52,8 @@
     near_rows, near_scale, second = lax.optimization_barrier((rows, scale, second))
     second_far = lax.ppermute(second, "xl", perm=SWAP)
     near = by_core(near_rows, near_scale, xl)
-    mixed = [
-        (near[:, :piece] + first_far).astype(jnp.bfloat16),
-        (near[:, piece:] + second_far).astype(jnp.bfloat16),
-    ]
-    return jnp.concatenate(mixed, axis=1)
+    mixed = near + jnp.concatenate([first_far, second_far], axis=1)
+    return mixed.astype(jnp.bfloat16)
 
 
 def solution(mesh):

time: 282 us -> 284 us (level)
    ppermute x1, waiting for transfers between devices: 9.76 us -> 26.7 us  [body(): first_far = lax.ppermute(first, 'xl', perm=SWAP)]
    ppermute x1, waiting for transfers between devices: 15.3 us -> 0.01 us  [body(): second_far = lax.ppermute(second, 'xl', perm=SWAP)]
  transfers between devices with their start and end apart: 7 -> 7, of which waited for: 4 -> 3; matrix products, arithmetic and copies ran while one was open for 11% -> 10% of each run, Pallas kernels for 0% -> 0%
where the time goes in v9:
time: 284 us; the launch traced here: 283 us
  waiting for transfers between devices  212 us (75%)
  matrix products  43.7 us (15%)
  between operations  13.6 us (5%)
  starting transfers between devices  7.25 us (3%)
  other arithmetic  7.2 us (3%)
    all_gather x1, waiting for transfers between devices, body(): w_full = lax.all_gather(pair, ('z', 'y'), axis=2, tiled=True)  177 us
    dot_general x6, matrix products, terms(): lax.dot_general(rows, w_part, (((2,), (2,)), ((0,), (0,))), preferred_ele...  35.5 us
    ppermute x1, waiting for transfers between devices, body(): first_far = lax.ppermute(first, 'xl', perm=SWAP)  26.7 us
    dot_general x1, matrix products, body(): lax.dot_general(pick.astype(hidden.dtype), hidden, (((2,), (0,)), ((), ()...  8.19 us
    ppermute x1, waiting for transfers between devices, body(): partner = lax.ppermute(down_weight, 'xh', perm=SWAP)  8.11 us
  transfers between devices with their start and end apart: 7, of which 3 were waited for; matrix products, arithmetic and copies ran while one was open for 10% of the time, Pallas kernels for 0%

profile of v9, /device:TPU:1, one launch (start us, length us, event | category | flops | bytes accessed | tf_op | source)
XLA Modules:
  0.0 283.4 jit_solution(7293120312424245613)
XLA Ops:
  6.5 0.0 copy-start
  6.5 0.0 all-gather.2.cloned.1.call-start
  6.5 3.6 %collective-permute-start = (bf16[2,48,2048]{2,1,0:T(8,128)(2,1)}, bf16[2,48,2048]{2,1,0:T(8,128)(2,1)S(1)}, u32[]{:S(2)}, u32[]{:S(2)}) collective-permute-start(bf16[2,48,2048]{2,1,0:T(8,128)(2,1)} %param.6), channel_id=1, source_target_pairs={{0,128},{128,0},{1,129},{129,1},{2,130},{130,2},{3,131},{131,3},{4... | collective-permute-start | bytes 1179656 | tf_op jit(solution)/shard_map/ppermute | solution.py:17
  10.1 8.1 %collective-permute-done = bf16[2,48,2048]{2,1,0:T(8,128)(2,1)S(1)} collective-permute-done((bf16[2,48,2048]{2,1,0:T(8,128)(2,1)}, bf16[2,48,2048]{2,1,0:T(8,128)(2,1)S(1)}, u32[]{:S(2)}, u32[]{:S(2)}) %collective-permute-start) | collective-permute-done | bytes 393248 | tf_op jit(solution)/shard_map/ppermute | solution.py:17
  18.2 1.9 pad_maximum_fusion
  20.2 0.0 all-gather.2.cloned.1.call-update
  20.2 0.0 copy-done
  20.2 0.1 broadcast_bitcast_fusion
  20.3 1.0 iota_compare_fusion
  21.3 1.5 fusion.14
  22.8 8.2 %fusion.16 = bf16[2,512,2048]{2,1,0:T(8,128)(2,1)} fusion(bf16[1024,2048]{1,0:T(8,128)(2,1)} %param.5, pred[2,1024]{1,0:T(4,128)(4,1)S(1)} %iota_compare_fusion.1, pred[512,1024]{1,0:T(8,128)(4,1)S(1)} %iota_compare_fusion), kind=kOutput, calls=%fused_computation.17 | convolution fusion | flops 4298113024 | bytes 8914944 | tf_op jit(solution)/shard_map/dot_general | solution.py:28
  31.0 176.8 %all-gather.2.cloned.1.call-done = bf16[2,2,1536,2048]{3,2,1,0:T(8,128)(2,1)} async-done(((bf16[2,2,48,2048]{3,2,1,0:T(8,128)(2,1)}), bf16[2,2,1536,2048]{3,2,1,0:T(8,128)(2,1)}) %all-gather.2.cloned.1.call-update) | async-done | bytes 25165840 | tf_op jit(solution)/shard_map/all_gather | solution.py:19
  207.8 0.0 copy-start.1
  207.8 3.9 %fusion.33 = f32[512,128]{1,0:T(8,128)S(1)} fusion(bf16[2,512,2048]{2,1,0:T(8,128)(2,1)} %fusion.16, bf16[2,2,1536,2048]{3,2,1,0:T(8,128)(2,1)} %all-gather.2.cloned.1.call-done, s32[]{:T(128)S(6)} %select_n.66, s32[]{:T(128)S(6)} %select_n.70, f32[2,512]{1,0:T(2,128)S(1)} %fusion.14), kind=kOutput, calls=%fused_computation.30 | convolution fusion | flops 537067520 | bytes 5509128 | tf_op jit(solution)/shard_map/dot_general | solution.py:38
  211.8 1.5 collective-permute-start.1
  213.2 0.0 copy-done.1
  213.2 2.5 fusion.32
  215.8 0.0 collective-permute-done.1
  215.8 6.1 %multiply_reduce_fusion.2 = f32[512,640]{1,0:T(8,128)S(1)} fusion(bf16[2,512,2048]{2,1,0:T(8,128)(2,1)S(1)} %copy-done.1, bf16[2,2,1536,2048]{3,2,1,0:T(8,128)(2,1)} %all-gather.2.cloned.1.call-done, s32[]{:T(128)S(6)} %select_n.66, s32[]{:T(128)S(6)} %select_n.74, f32[2,512]{1,0:T(2,128)S(1)} %fusion.14), kind=kOutput, calls=%fused_computation.20 | convolution fusion | flops 2685337600 | bytes 10752008 | tf_op jit(solution)/shard_map/dot_general | solution.py:38
  222.0 0.3 collective-permute-start.2
  222.3 0.0 copy-start.2
  222.3 7.5 %multiply_reduce_fusion.3 = f32[512,640]{1,0:T(8,128)S(1)} fusion(bf16[2,512,2048]{2,1,0:T(8,128)(2,1)} %fusion.16, bf16[2,2,1536,2048]{3,2,1,0:T(8,128)(2,1)} %all-gather.2.cloned.1.call-done, s32[]{:T(128)S(6)} %select_n.66, s32[]{:T(128)S(6)} %select_n.72, f32[2,512]{1,0:T(2,128)S(1)} %fusion.14), kind=kOutput, calls=%fused_computation.21 | convolution fusion | flops 2685337600 | bytes 10752008 | tf_op jit(solution)/shard_map/dot_general | solution.py:38
  229.8 0.0 collective-permute-done.2
  229.8 0.2 add.101
  230.0 0.0 copy-done.2
  230.0 7.7 %multiply_reduce_fusion = f32[512,768]{1,0:T(8,128)} fusion(f32[2,512]{1,0:T(2,128)S(1)} %fusion.14, bf16[2,512,2048]{2,1,0:T(8,128)(2,1)S(1)} %copy-done.2, bf16[2,2,1536,2048]{3,2,1,0:T(8,128)(2,1)} %all-gather.2.cloned.1.call-done, s32[]{:T(128)S(6)} %select_n.77, s32[]{:T(128)S(6)} %select_n.79), kind=kOutput, calls=%fused_computation.18 | convolution fusion | flops 3222405120 | bytes 12062728 | tf_op jit(solution)/shard_map/dot_general | solution.py:38
  237.6 0.5 collective-permute-start.3
  238.1 1.2 collective-permute-start.5
  239.3 0.3 collective-permute-start.4
  239.6 7.8 %multiply_reduce_fusion.1 = f32[512,768]{1,0:T(8,128)S(1)} fusion(f32[2,512]{1,0:T(2,128)S(1)} %fusion.14, bf16[2,512,2048]{2,1,0:T(8,128)(2,1)} %fusion.16, bf16[2,2,1536,2048]{3,2,1,0:T(8,128)(2,1)} %all-gather.2.cloned.1.call-done, s32[]{:T(128)S(6)} %select_n.77, s32[]{:T(128)S(6)} %select_n.78), kind=kOutput, calls=%fused_computation.19 | convolution fusion | flops 3222405120 | bytes 12062728 | tf_op jit(solution)/shard_map/dot_general | solution.py:38
  247.3 26.7 %collective-permute-done.4 = f32[512,128]{1,0:T(8,128)S(1)} collective-permute-done((f32[512,128]{1,0:T(8,128)S(1)}, f32[512,128]{1,0:T(8,128)S(1)}, u32[]{:S(2)}, u32[]{:S(2)}) %collective-permute-start.4) | collective-permute-done | bytes 262176 | tf_op jit(solution)/shard_map/ppermute | solution.py:49
  274.0 0.0 collective-permute-done.5
  274.0 0.0 collective-permute-done.3
  274.0 2.5 fusion.23
  (2 shorter events, 0.0 us)
Async XLA Ops:
  6.5 13.7 %copy-start = (s32[8]{0:T(128)S(1)}, s32[8]{0:T(128)}, u32[]{:S(2)}) copy-start(s32[8]{0:T(128)} %param.7) | copy-start | bytes 100
  6.5 201.3 %all-gather.2.cloned.1.call-start = ((), (), s32[]{:S(2)}) async-start(), calls=%async_computation | async-start | bytes 25952256 | tf_op jit(solution)/shard_map/all_gather | solution.py:19
  6.5 11.7 %collective-permute-start = (bf16[2,48,2048]{2,1,0:T(8,128)(2,1)}, bf16[2,48,2048]{2,1,0:T(8,128)(2,1)S(1)}, u32[]{:S(2)}, u32[]{:S(2)}) collective-permute-start(bf16[2,48,2048]{2,1,0:T(8,128)(2,1)} %param.6), channel_id=1, source_target_pairs={{0,128},{128,0},{1,129},{129,1},{2,130},{130,2},{3,131},{131,3},{4... | collective-permute-start | bytes 1179656 | tf_op jit(solution)/shard_map/ppermute | solution.py:17
  207.8 5.4 %copy-start.1 = (bf16[2,512,2048]{2,1,0:T(8,128)(2,1)S(1)}, bf16[2,512,2048]{2,1,0:T(8,128)(2,1)}, u32[]{:S(2)}) copy-start(bf16[2,512,2048]{2,1,0:T(8,128)(2,1)} %fusion.16) | copy-start | bytes 12582916
  211.8 4.0 %collective-permute-start.1 = (f32[512,128]{1,0:T(8,128)S(1)}, f32[512,128]{1,0:T(8,128)S(1)}, u32[]{:S(2)}, u32[]{:S(2)}) collective-permute-start(f32[512,128]{1,0:T(8,128)S(1)} %fusion.33), channel_id=1, source_target_pairs={{0,1},{1,0},{2,3},{3,2},{4,5},{5,4},{6,7},{7,6},{8,9},{9,8},{10,11... | collective-permute-start | bytes 786440 | tf_op jit(solution)/shard_map/ppermute | solution.py:44
  222.0 7.8 %collective-permute-start.2 = (f32[512,640]{1,0:T(8,128)S(1)}, f32[512,640]{1,0:T(8,128)S(1)}, u32[]{:S(2)}, u32[]{:S(2)}) collective-permute-start(f32[512,640]{1,0:T(8,128)S(1)} %multiply_reduce_fusion.2), channel_id=1, source_target_pairs={{0,1},{1,0},{2,3},{3,2},{4,5},{5,4},{6,7},{7,6},{8,9},{9,8},{10,11... | collective-permute-start | bytes 3932168 | tf_op jit(solution)/shard_map/ppermute | solution.py:44
  222.3 7.7 %copy-start.2 = (bf16[2,512,2048]{2,1,0:T(8,128)(2,1)S(1)}, bf16[2,512,2048]{2,1,0:T(8,128)(2,1)}, u32[]{:S(2)}) copy-start(bf16[2,512,2048]{2,1,0:T(8,128)(2,1)} %fusion.16) | copy-start | bytes 12582916
  237.6 36.4 %collective-permute-start.3 = (f32[512,768]{1,0:T(8,128)}, f32[512,768]{1,0:T(8,128)S(1)}, u32[]{:S(2)}, u32[]{:S(2)}) collective-permute-start(f32[512,768]{1,0:T(8,128)} %multiply_reduce_fusion), channel_id=1, source_target_pairs={{0,1},{1,0},{2,3},{3,2},{4,5},{5,4},{6,7},{7,6},{8,9},{9,8},{10,11... | collective-permute-start | bytes 4718600 | tf_op jit(solution)/shard_map/ppermute | solution.py:44
  238.1 35.9 %collective-permute-start.5 = (f32[512,640]{1,0:T(8,128)S(1)}, f32[512,640]{1,0:T(8,128)}, u32[]{:S(2)}, u32[]{:S(2)}) collective-permute-start(f32[512,640]{1,0:T(8,128)S(1)} %add.101), channel_id=1, source_target_pairs={{0,2},{2,0},{1,3},{3,1},{4,6},{6,4},{5,7},{7,5},{8,10},{10,8},{9,1... | collective-permute-start | bytes 3932168 | tf_op jit(solution)/shard_map/ppermute | solution.py:53
  239.3 34.7 %collective-permute-start.4 = (f32[512,128]{1,0:T(8,128)S(1)}, f32[512,128]{1,0:T(8,128)S(1)}, u32[]{:S(2)}, u32[]{:S(2)}) collective-permute-start(f32[512,128]{1,0:T(8,128)S(1)} %add.96), channel_id=1, source_target_pairs={{0,2},{2,0},{1,3},{3,1},{4,6},{6,4},{5,7},{7,5},{8,10},{10,8},{9,1... | collective-permute-start | bytes 786440 | tf_op jit(solution)/shard_map/ppermute | solution.py:49
Sparse Core Ops, SparseCore 0:
  20.3 187.4 all-gather.1
